TPU v7x, 128 devices: a whole 4x4x4 slice. The times are simulated.
128 devices in a mesh: leaf: 16 (over y, z), ctx: 8 (over x, core).
Axes of the slice: x: 4, y: 4, z: 4, core: 2. Of those that a mesh axis runs over, the one named last changes fastest.
Arguments:
- query_key_value_rows: bfloat16 [16384, 7168], P(('leaf', 'ctx')), may hold values from -6 to 6
- cotangent: bfloat16 [16384, 5120], P(('leaf', 'ctx')), may hold values from -6 to 6
- out_weight: bfloat16 [5120, 5120], P('ctx'), may hold values from -0.078125 to 0.078125
- parents: int32 [16, 8], P('leaf'), may hold values from 0 to 6, as said below
- rollout_spans: int32 [16384], P('leaf'), may hold values from 64 to 4096
Outputs:
- qkv_grad: bfloat16 [16384, 7168], P(('leaf', 'ctx'))
- weight_grad: bfloat16 [5120, 5120], P('ctx')
Inputs may be any that keep to these rules, and one draw needn't show every extreme that they name: parents[t, 0] = 0, every later block's parent is an earlier block of the same tree, and the last block's parent is the block just before it.
All inputs are finite; a program needn't handle non-finite values.
Results may differ from a plain program's by a relative error of at most 0.012.
The roundings to bfloat16 on the way count: a program that leaves them out, or rounds other values in their place, can miss the bound.
Values may be sent and summed in bfloat16 or wider, within the bound.
No kernel may reach another device: no remote copies, remote signals or barrier semaphores. Data moves between devices by JAX's collectives and lax.ppermute only.
A program may use at most 192 MiB of HBM per device.

v0:
```python
import math

import jax
import jax.numpy as jnp
from jax import lax
from jax.sharding import PartitionSpec as P

QUERY_HEADS = 40
KEY_VALUE_HEADS = 8
HEAD_SIZE = 128
BLK = 128


log_base = 1024.0


def ancestors(parents):
    number = parents.shape[0]
    indices = jnp.arange(number, dtype=jnp.int32)

    def advance(iteration, state):
        current, reached = state
        current = jnp.sum(
            jnp.where(current[:, None] == indices[None, :], parents[None, :], 0), axis=1
        )
        return (current, reached | (current[:, None] == indices[None, :]))

    return lax.fori_loop(0, number, advance, (indices, indices[:, None] == indices[None, :]))[1]


def token_mask(reached, first_row, query_count, key_count):
    query_pos = first_row + jnp.arange(query_count, dtype=jnp.int32)
    key_pos = jnp.arange(key_count, dtype=jnp.int32)
    block_part = reached[first_row // BLK : (first_row + query_count) // BLK, : key_count // BLK]
    expanded = jnp.repeat(jnp.repeat(block_part, BLK, axis=0), BLK, axis=1)
    same_block = (query_pos // BLK)[:, None] == (key_pos // BLK)[None, :]
    return expanded & (jnp.logical_not(same_block) | (key_pos[None, :] <= query_pos[:, None]))


def span_softness(rollout_spans):
    return jnp.log(rollout_spans.astype(jnp.float32)) * (
        1.0 / (math.log(log_base) * math.sqrt(HEAD_SIZE))
    )


def contract_rows(left, right):
    return lax.dot_general(
        left, right, (((0,), (0,)), ((), ())), preferred_element_type=jnp.float32
    )


def contract_cols(left, right):
    return lax.dot_general(
        left, right, (((1,), (1,)), ((), ())), preferred_element_type=jnp.float32
    )


def local(query_key_value_rows, cotangent, out_weight, parents, rollout_spans):
    queries_per_group = QUERY_HEADS // KEY_VALUE_HEADS
    head_rows = lax.all_to_all(query_key_value_rows, "ctx", split_axis=1, concat_axis=0, tiled=True)
    tree_len = head_rows.shape[0]
    kv_local = head_rows.shape[1] // ((queries_per_group + 2) * HEAD_SIZE)
    heads_local = kv_local * queries_per_group
    grouped = head_rows.reshape(tree_len, kv_local, queries_per_group + 2, HEAD_SIZE)
    asking_matrix = grouped[:, :, :queries_per_group]
    lookup_matrix = grouped[:, :, queries_per_group]
    value_rows = grouped[:, :, queries_per_group + 1]
    softness_multiplier = span_softness(rollout_spans)
    reached = ancestors(parents[0])
    block_len = min(512, tree_len)
    block_total = tree_len // block_len
    masks = []
    total_parts = []
    attended_parts = []
    for block_id in range(block_total):
        opening_slot = block_id * block_len
        closing_slot = opening_slot + block_len
        allowed = token_mask(reached, opening_slot, block_len, closing_slot)
        masks.append(allowed)
        attention_logits = jnp.einsum(
            "zpyr,kpr->pyzk",
            asking_matrix[opening_slot:closing_slot],
            lookup_matrix[:closing_slot],
            preferred_element_type=jnp.float32,
        )
        attention_logits = jnp.where(
            allowed[None, None],
            attention_logits * softness_multiplier[opening_slot:closing_slot][None, None, :, None],
            -jnp.inf,
        )
        peak_score = jnp.max(attention_logits, axis=-1, keepdims=True)
        log_total = peak_score + jnp.log(
            jnp.sum(jnp.exp(attention_logits - peak_score), axis=-1, keepdims=True)
        )
        weights_low = jnp.exp(attention_logits - log_total).astype(jnp.bfloat16)
        attended_parts.append(
            jnp.einsum(
                "gjts,sgd->tgjd",
                weights_low,
                value_rows[:closing_slot],
                preferred_element_type=jnp.float32,
            ).astype(jnp.bfloat16)
        )
        total_parts.append(log_total[..., 0])
    attended = jnp.concatenate(attended_parts, axis=0)
    log_totals = jnp.concatenate(total_parts, axis=2)
    flat_out = attended.reshape(tree_len, heads_local * HEAD_SIZE)
    shard_rows = lax.all_gather(cotangent, "ctx", axis=0, tiled=True)
    weight_low = contract_rows(flat_out, shard_rows).astype(jnp.bfloat16)
    weight_low, shard_rows = lax.optimization_barrier((weight_low, shard_rows))
    weight_total = lax.psum(weight_low, "leaf")
    def backward_part():
        output_gradient = contract_cols(shard_rows, out_weight).astype(jnp.bfloat16)
        asking_heads = asking_matrix.reshape(tree_len, heads_local, HEAD_SIZE)
        attended_heads = attended.reshape(tree_len, heads_local, HEAD_SIZE)
        grad_heads = output_gradient.reshape(tree_len, heads_local, HEAD_SIZE)
        totals_heads = log_totals.reshape(heads_local, tree_len)

        def one_head(head_id, carry):
            key_acc, value_acc, query_grad = carry
            kv_id = head_id // queries_per_group
            keys_all = lax.dynamic_index_in_dim(lookup_matrix, kv_id, axis=1, keepdims=False)
            values_all = lax.dynamic_index_in_dim(value_rows, kv_id, axis=1, keepdims=False)
            query_all = lax.dynamic_index_in_dim(asking_heads, head_id, axis=1, keepdims=False)
            grad_all = lax.dynamic_index_in_dim(grad_heads, head_id, axis=1, keepdims=False)
            own_all = lax.dynamic_index_in_dim(attended_heads, head_id, axis=1, keepdims=False)
            totals_all = lax.dynamic_index_in_dim(totals_heads, head_id, axis=0, keepdims=False)
            key_now = lax.dynamic_index_in_dim(key_acc, kv_id, axis=1, keepdims=False)
            value_now = lax.dynamic_index_in_dim(value_acc, kv_id, axis=1, keepdims=False)
            query_blocks = []
            for block_id in range(block_total):
                opening_slot = block_id * block_len
                closing_slot = opening_slot + block_len
                query_now = query_all[opening_slot:closing_slot]
                keys_now = keys_all[:closing_slot]
                values_now = values_all[:closing_slot]
                line_multiplier = softness_multiplier[opening_slot:closing_slot][:, None]
                attention_logits = jnp.where(
                    masks[block_id], contract_cols(query_now, keys_now) * line_multiplier, -jnp.inf
                )
                attention_probabilities = jnp.exp(
                    attention_logits - totals_all[opening_slot:closing_slot][:, None]
                )
                grad_rows = grad_all[opening_slot:closing_slot]
                own_rows = own_all[opening_slot:closing_slot]
                probability_cotangent = contract_cols(grad_rows, values_now)
                middle_point = jnp.sum(
                    grad_rows.astype(jnp.float32) * own_rows.astype(jnp.float32), axis=1
                )
                logit_cotangent = (
                    attention_probabilities
                    * (probability_cotangent - middle_point[:, None])
                    * line_multiplier
                ).astype(jnp.bfloat16)
                query_blocks.append(
                    jnp.dot(logit_cotangent, keys_now, preferred_element_type=jnp.float32).astype(
                        jnp.bfloat16
                    )
                )
                key_now = key_now.at[:closing_slot].add(contract_rows(logit_cotangent, query_now))
                value_now = value_now.at[:closing_slot].add(
                    contract_rows(attention_probabilities.astype(jnp.bfloat16), grad_rows)
                )
            key_acc = lax.dynamic_update_index_in_dim(key_acc, key_now, kv_id, axis=1)
            value_acc = lax.dynamic_update_index_in_dim(value_acc, value_now, kv_id, axis=1)
            query_grad = lax.dynamic_update_index_in_dim(
                query_grad, jnp.concatenate(query_blocks, axis=0), head_id, axis=1
            )
            return key_acc, value_acc, query_grad

        key_acc, value_acc, query_grad = lax.fori_loop(
            0,
            heads_local,
            one_head,
            (
                jnp.zeros((tree_len, kv_local, HEAD_SIZE), jnp.float32),
                jnp.zeros((tree_len, kv_local, HEAD_SIZE), jnp.float32),
                jnp.zeros((tree_len, heads_local, HEAD_SIZE), jnp.bfloat16),
            ),
        )
        query_grad = query_grad.reshape(tree_len, kv_local, queries_per_group, HEAD_SIZE)
        gradients = jnp.concatenate(
            [
                query_grad,
                key_acc.astype(jnp.bfloat16)[:, :, None],
                value_acc.astype(jnp.bfloat16)[:, :, None],
            ],
            axis=2,
        )
        gradients = gradients.reshape(tree_len, kv_local * (queries_per_group + 2) * HEAD_SIZE)
        return gradients

    def no_part():
        return jnp.zeros((tree_len, kv_local * (queries_per_group + 2) * HEAD_SIZE), jnp.bfloat16)

    gradients = lax.cond(lax.axis_index("ctx") >= 0, backward_part, no_part)
    returned = lax.all_to_all(gradients, "ctx", split_axis=0, concat_axis=1, tiled=True)
    return (returned, weight_total)


def solution(mesh):
    placed = (
        P(("leaf", "ctx"), None),
        P(("leaf", "ctx"), None),
        P("ctx", None),
        P("leaf", None),
        P("leaf"),
    )
    return jax.shard_map(
        local,
        mesh=mesh,
        in_specs=placed,
        out_specs=(P(("leaf", "ctx"), None), P("ctx", None)),
        check_vma=False,
    )
```

profile of v0, /device:TPU:1, one launch (start us, length us, event | category | flops | bytes accessed | tf_op | source)
XLA Modules:
  0.0 262.1 jit_solution(4626520845996293652)
XLA Ops:
  7.9 3.9 %copy.61 = bf16[128,7168]{0,1:T(8,128)(2,1)} copy(bf16[128,7168]{1,0:T(8,128)(2,1)} %param.23) | data formatting | bytes 3670016 | tf_op args[0]
  11.8 5.9 %all-to-all-start = ((bf16[128,8,896]{0,2,1:T(8,128)(2,1)}), bf16[128,8,896]{0,2,1:T(8,128)(2,1)S(1)}, u32[]{:S(2)}, u32[]{:S(2)}) async-start(bf16[128,8,896]{0,2,1:T(8,128)(2,1)} %bitcast.303), calls=%async_computation | async-start | bytes 3670016 | tf_op jit(solution)/shard_map/all_to_all | solution.py:60
  17.7 2.2 while.53
  21.9 32.5 %all-to-all-done = bf16[128,8,896]{0,2,1:T(8,128)(2,1)S(1)} async-done(((bf16[128,8,896]{0,2,1:T(8,128)(2,1)}), bf16[128,8,896]{0,2,1:T(8,128)(2,1)S(1)}, u32[]{:S(2)}, u32[]{:S(2)}) %all-to-all-start) | async-done | bytes 1835040 | tf_op jit(solution)/shard_map/all_to_all | solution.py:60
  54.4 2.4 copy.62
  56.8 2.7 %reshape.561 = bf16[1024,1,7,128]{0,3,2,1:T(8,128)(2,1)S(1)} reshape(bf16[8,128,896]{1,0,2:T(8,128)(2,1)} %copy.62) | data formatting | bytes 3670016 | tf_op jit(solution)/shard_map/reshape | solution.py:64
  61.7 1.8 fusion.34
  63.5 2.2 exponential_reduce_fusion
  65.8 1.9 fusion.55
  67.7 3.9 %fusion.52 = bf16[512,1,5,128]{3,0,2,1:T(8,128)(2,1)S(1)} fusion(f32[1024,512,5]{1,0,2:T(8,128)S(1)} %get-tuple-element.730, f32[5,512]{1,0:T(8,128)S(1)} %log_add_fusion, f32[512]{0:T(512)S(1)} %get-tuple-element.728, pred[512,1024]{0,1:T(8,128)(4,1)S(1)} %fusion.45, bf16[1024,1,7,128]{0,3,2,1:T(8,128)(2,1)S(1)} %reshape.561), kind=kOutput, calls=%fused_computation.87 | convolution fusion | flops 681902080 | bytes 11945984 | tf_op jit(solution)/shard_map/gjts,sgd->tgjd/dot_general | solution.py:97
  71.7 1.5 copy.73
  73.1 12.5 %all-gather.2.cloned.1.call-done = bf16[1024,5120]{1,0:T(8,128)(2,1)} async-done(((bf16[128,5120]{1,0:T(8,128)(2,1)}), bf16[1024,5120]{1,0:T(8,128)(2,1)}) %all-gather.2.cloned.1.call-update) | async-done | bytes 10485776 | tf_op jit(solution)/shard_map/all_gather | solution.py:108
  85.6 11.7 %convolution_convert_fusion.3 = bf16[640,5120]{1,0:T(8,128)(2,1)} fusion(bf16[1024,640]{0,1:T(8,128)(2,1)} %bitcast.309, bf16[1024,5120]{1,0:T(8,128)(2,1)} %all-gather.2.cloned.1.call-done), kind=kOutput, calls=%fused_computation.69 | convolution fusion | flops 6714163200 | bytes 18350080 | tf_op jit(solution)/shard_map/dot_general | solution.py:47
  99.4 1.4 pad_maximum_fusion.2
  100.8 1.6 broadcast_in_dim.151
  102.3 2.4 broadcast_in_dim.155
  107.0 1.6 le.57
  108.6 103.3 %conditional.1 = (bf16[1024,896]{0,1:T(8,128)(2,1)S(1)}) conditional(s32[]{:T(128)} %convert_element_type.154, () %tuple.93, (bf16[1024,1,1,128]{3,0,2,1:T(8,128)(2,1)S(1)}, bf16[1024,1,1,128]{3,0,2,1:T(8,128)(2,1)S(1)}, bf16[1024,1,7,128]{0,3,2,1:T(8,128)(2,1)}, bf16[1024,5120]{1,0:T(8,128)(2,1)}, bf16[640,5120]{1,0:T(8,128)(2,1)}, ...), branch_computations={%region_7.8_spmd, %region_8.13_spmd} | conditional | flops 7731805184 | bytes 92977760 | solution.py:196
  108.6 3.3 %bitcast_and_fusion.1 = pred[512,512]{1,0:T(32,128)(4,1)} fusion(pred[64,8,4,128]{3,2,1,0:T(4,128)(4,1)S(1)} %bitcast.313, s32[512,512]{1,0:T(8,128)} %get-tuple-element.514, s32[512,512]{1,0:T(8,128)} %get-tuple-element.515, s32[512]{0:T(512)S(1)} %get-tuple-element.513), kind=kLoop, calls=%fused_computation.57 | loop fusion | flops 1310720 | bytes 2623488 | tf_op jit(solution)/shard_map/and | solution.py:37
  111.9 1.6 bitcast_and_fusion
  113.5 12.7 %convolution_convert_fusion.2 = bf16[1024,640]{0,1:T(8,128)(2,1)} fusion(bf16[1024,5120]{1,0:T(8,128)(2,1)} %get-tuple-element.517, bf16[640,5120]{1,0:T(8,128)(2,1)} %get-tuple-element.538), kind=kOutput, calls=%fused_computation.55 | convolution fusion | flops 6711541760 | bytes 18350080 | tf_op jit(solution)/shard_map/cond/branch_1_fun/dot_general | solution.py:53
  126.2 3.2 %copy.57 = bf16[1024,5,128]{2,1,0:T(8,128)(2,1)S(1)} copy(bf16[1024,5,128]{0,2,1:T(8,128)(2,1)} %bitcast.310) | data formatting | bytes 2621440 | tf_op jit(solution)/shard_map/cond/branch_1_fun/while | solution.py:171
  129.4 3.8 %copy.74 = bf16[1024,1,7,128]{3,0,2,1:T(8,128)(2,1)} copy(bf16[1024,1,7,128]{0,3,2,1:T(8,128)(2,1)} %get-tuple-element.668) | data formatting | bytes 3670016 | tf_op jit(solution)/shard_map
  133.2 2.5 slice_bitcast_fusion
  135.7 73.5 %while.52 = (s32[]{:T(128)}, f32[1024,1,128]{2,0,1:T(8,128)S(1)}, f32[1024,1,128]{2,0,1:T(8,128)S(1)}, bf16[1024,5,128]{0,2,1:T(8,128)(2,1)}, bf16[1024,5,128]{2...) while((s32[]{:T(128)}, f32[1024,1,128]{2,0,1:T(8,128)S(1)}, ...), condition=%wide.region_12.12_spmd, body=%wide.region_9.11_spmd.sunk | while | flops 1014496256 | bytes 31625536 | solution.py:171
  137.0 1.3 fusion.126
  138.9 1.2 fusion.127
  140.5 1.3 fusion.129
  142.0 1.6 subtract_exponential_fusion.2
  144.6 1.4 fusion.130
  147.2 1.8 copy.99
  149.0 1.7 constant_dynamic-update-slice_fusion.2
  151.6 1.3 fusion.126
  153.5 1.3 fusion.127
  155.1 1.3 fusion.129
  156.7 1.6 subtract_exponential_fusion.2
  159.2 1.4 fusion.130
  161.8 1.8 copy.99
  163.6 1.7 constant_dynamic-update-slice_fusion.2
  166.2 1.3 fusion.126
  168.1 1.3 fusion.127
  169.7 1.3 fusion.129
  171.3 1.6 subtract_exponential_fusion.2
  173.8 1.4 fusion.130
  176.4 1.8 copy.99
  178.2 1.6 constant_dynamic-update-slice_fusion.2
  180.8 1.3 fusion.126
  182.7 1.2 fusion.127
  184.3 1.3 fusion.129
  185.9 1.6 subtract_exponential_fusion.2
  188.4 1.4 fusion.130
  191.0 1.8 copy.99
  192.8 1.7 constant_dynamic-update-slice_fusion.2
  195.6 1.3 fusion.126
  199.1 1.3 fusion.129
  200.6 1.6 subtract_exponential_fusion.2
  203.2 1.4 fusion.130
  205.7 1.8 copy.99
  207.5 1.7 constant_dynamic-update-slice_fusion.2
  213.1 3.1 %copy.75 = bf16[1024,896]{1,0:T(8,128)(2,1)S(1)} copy(bf16[1024,896]{0,1:T(8,128)(2,1)} %copy-done.7) | data formatting | bytes 3670016 | tf_op jit(solution)/shard_map/cond | solution.py:196
  216.2 26.9 %all_to_all.35 = bf16[8,128,896]{2,1,0:T(8,128)(2,1)} all-to-all(bf16[8,128,896]{2,1,0:T(8,128)(2,1)S(1)} %bitcast.304), channel_id=1, replica_groups=mesh['leaf'=16,'ctx'=8] {'ctx'}, dimensions={0} | all-to-all | bytes 3670016 | tf_op jit(solution)/shard_map/all_to_all | solution.py:197
  243.1 3.2 %copy.76 = bf16[8,128,896]{1,2,0:T(8,128)(2,1)S(1)} copy(bf16[8,128,896]{2,1,0:T(8,128)(2,1)} %all_to_all.35) | data formatting | bytes 3670016 | tf_op jit(solution)/shard_map/all_to_all | solution.py:197
  246.3 2.9 %copy.77 = bf16[128,7168]{1,0:T(8,128)(2,1)} copy(bf16[128,7168]{0,1:T(8,128)(2,1)S(1)} %bitcast.305) | data formatting | bytes 3670016
  249.2 6.1 %copy.133 = bf16[640,5120]{1,0:T(8,128)(2,1)} copy(bf16[640,5120]{1,0:T(8,128)(2,1)} %all-reduce.2.cloned.1.call-done) | data formatting | bytes 13107200
  (177 shorter events, 37.7 us)
Async XLA Ops:
  7.2 78.5 %all-gather.2.cloned.1.call-start = ((), (), s32[]{:S(2)}) async-start(), calls=%async_computation.2 | async-start | bytes 11796480 | tf_op jit(solution)/shard_map/all_gather | solution.py:108
  11.8 6.0 %copy-start.15 = (s32[1,8]{1,0:T(1,128)S(1)}, s32[1,8]{1,0:T(1,128)}, u32[]{:S(2)}) copy-start(s32[1,8]{1,0:T(1,128)} %param.26) | copy-start | bytes 100
  11.8 10.1 %copy-start.14 = (s32[1024]{0:T(1024)S(1)}, s32[1024]{0:T(1024)}, u32[]{:S(2)}) copy-start(s32[1024]{0:T(1024)} %param.27) | copy-start | bytes 12292
  11.8 42.6 %all-to-all-start = ((bf16[128,8,896]{0,2,1:T(8,128)(2,1)}), bf16[128,8,896]{0,2,1:T(8,128)(2,1)S(1)}, u32[]{:S(2)}, u32[]{:S(2)}) async-start(bf16[128,8,896]{0,2,1:T(8,128)(2,1)} %bitcast.303), calls=%async_computation | async-start | bytes 3670016 | tf_op jit(solution)/shard_map/all_to_all | solution.py:60
  17.7 231.5 %all-reduce.2.cloned.1.call-start = ((), (), s32[]{:S(2)}) async-start(), calls=%async_computation.3 | async-start | bytes 13107200 | tf_op jit(solution)/shard_map/psum | solution.py:111
  20.6 0.6 copy-start.12
  59.6 37.8 %copy-start.3 = (bf16[1024,1,7,128]{0,3,2,1:T(8,128)(2,1)}, bf16[1024,1,7,128]{0,3,2,1:T(8,128)(2,1)S(1)}, u32[]{:S(2)}) copy-start(bf16[1024,1,7,128]{0,3,2,1:T(8,128)(2,1)S(1)} %reshape.561) | copy-start | bytes 5505028
  61.7 4.1 %copy-start.10 = (f32[5,512]{1,0:T(8,128)}, f32[5,512]{1,0:T(8,128)S(1)}, u32[]{:S(2)}) copy-start(f32[5,512]{1,0:T(8,128)S(1)} %log_add_fusion.1) | copy-start | bytes 30724
  65.8 1.9 copy-start.11
  104.8 3.8 %copy-start.13 = (s32[512]{0:T(512)S(1)}, s32[512]{0:T(512)}, u32[]{:S(2)}) copy-start(s32[512]{0:T(512)} %copy-done.12) | copy-start | bytes 6148
  108.6 4.9 %copy-start = (bf16[1024,1,1,128]{3,0,2,1:T(8,128)(2,1)}, bf16[1024,1,1,128]{3,0,2,1:T(8,128)(2,1)S(1)}, u32[]{:S(2)}) copy-start(bf16[1024,1,1,128]{3,0,2,1:T(8,128)(2,1)S(1)} %get-tuple-element.519) | copy-start | bytes 786436 | tf_op jit(solution)/shard_map/cond
  108.6 4.9 %copy-start.4 = (bf16[1024,1,5,128]{3,0,2,1:T(8,128)(2,1)}, bf16[1024,1,5,128]{3,0,2,1:T(8,128)(2,1)S(1)}, u32[]{:S(2)}) copy-start(bf16[1024,1,5,128]{3,0,2,1:T(8,128)(2,1)S(1)} %get-tuple-element.520) | copy-start | bytes 3932164 | tf_op jit(solution)/shard_map/cond
  108.6 3.3 %copy-start.8 = (pred[512,8,128]{2,1,0:T(8,128)(4,1)S(1)}, pred[512,8,128]{2,1,0:T(8,128)(4,1)}, u32[]{:S(2)}) copy-start(pred[512,8,128]{2,1,0:T(8,128)(4,1)} %get-tuple-element.521) | copy-start | bytes 1572868 | tf_op jit(solution)/shard_map/cond
  108.6 3.3 %copy-start.6 = (s32[512,1024]{1,0:T(8,128)S(1)}, s32[512,1024]{1,0:T(8,128)}, u32[]{:S(2)}) copy-start(s32[512,1024]{1,0:T(8,128)} %get-tuple-element.524) | copy-start | bytes 6291460 | tf_op jit(solution)/shard_map/cond
  136.0 1.0 copy-start.5
  138.3 1.8 copy-start.1
  138.9 3.2 %copy-start.2 = (pred[512,1024]{1,0:T(32,128)(4,1)S(1)}, pred[512,1024]{1,0:T(32,128)(4,1)}, u32[]{:S(2)}) copy-start(pred[512,1024]{1,0:T(32,128)(4,1)} %get-tuple-element.895) | copy-start | bytes 1572868 | tf_op jit(solution)/shard_map/cond/branch_1_fun/while
  150.6 1.0 copy-start.5
  153.0 1.8 copy-start.1
  153.5 3.2 %copy-start.2 = (pred[512,1024]{1,0:T(32,128)(4,1)S(1)}, pred[512,1024]{1,0:T(32,128)(4,1)}, u32[]{:S(2)}) copy-start(pred[512,1024]{1,0:T(32,128)(4,1)} %get-tuple-element.895) | copy-start | bytes 1572868 | tf_op jit(solution)/shard_map/cond/branch_1_fun/while
  165.2 1.0 copy-start.5
  167.6 1.8 copy-start.1
  168.1 3.2 %copy-start.2 = (pred[512,1024]{1,0:T(32,128)(4,1)S(1)}, pred[512,1024]{1,0:T(32,128)(4,1)}, u32[]{:S(2)}) copy-start(pred[512,1024]{1,0:T(32,128)(4,1)} %get-tuple-element.895) | copy-start | bytes 1572868 | tf_op jit(solution)/shard_map/cond/branch_1_fun/while
  179.8 1.0 copy-start.5
  182.2 1.8 copy-start.1
  182.7 3.2 %copy-start.2 = (pred[512,1024]{1,0:T(32,128)(4,1)S(1)}, pred[512,1024]{1,0:T(32,128)(4,1)}, u32[]{:S(2)}) copy-start(pred[512,1024]{1,0:T(32,128)(4,1)} %get-tuple-element.895) | copy-start | bytes 1572868 | tf_op jit(solution)/shard_map/cond/branch_1_fun/while
  194.5 1.0 copy-start.5
  196.9 1.8 copy-start.1
  197.5 3.2 %copy-start.2 = (pred[512,1024]{1,0:T(32,128)(4,1)S(1)}, pred[512,1024]{1,0:T(32,128)(4,1)}, u32[]{:S(2)}) copy-start(pred[512,1024]{1,0:T(32,128)(4,1)} %get-tuple-element.895) | copy-start | bytes 1572868 | tf_op jit(solution)/shard_map/cond/branch_1_fun/while
  209.2 1.5 copy-start.9
  211.9 1.2 copy-start.7
Sparse Core Ops, SparseCore 0:
  9.7 75.9 all-gather.1
  97.5 124.9 all-reduce.1
where the time goes:
time: 264 us; the launch traced here: 262 us
  matrix products  72.5 us (27%)
  local copies, waits for them, and re-layouts  71.9 us (27%)
  waiting for transfers between devices  45.7 us (17%)
  blocking collectives  26.9 us (10%)
  other arithmetic  23.8 us (9%)
  between operations  14.3 us (5%)
  starting transfers between devices  5.97 us (2%)
    all_to_all x1, waiting for transfers between devices, local(): lax.all_to_all(query_key_value_rows, 'ctx', split_axis=1, concat_axis=0,...  32.5 us
    dot_general x21, matrix products, contract_cols(): lax.dot_general(left, right, (((1,), (1,)), ((), ())), preferred_element_...  31.1 us
    dot_general x21, matrix products, contract_rows(): lax.dot_general(left, right, (((0,), (0,)), ((), ())), preferred_element_...  29.1 us
    all_to_all x1, blocking collectives, local(): lax.all_to_all(gradients, 'ctx', split_axis=0, concat_axis=1, tiled=True)  26.9 us
    dynamic_update_slice x10, local copies, waits for them, and re-layouts, one_head(): lax.dynamic_update_index_in_dim(query_grad, jnp.concatenate(query_blocks,...  17.5 us
    unnamed x23, local copies, waits for them, and re-layouts  16.2 us
    all_gather x1, waiting for transfers between devices, local(): shard_rows = lax.all_gather(cotangent, 'ctx', axis=0, tiled=True)  12.5 us
    reduce_sum x5, other arithmetic, one_head(): jnp.sum(grad_rows.astype(jnp.float32) * own_rows.astype(jnp.float32), axi...  6.25 us
  transfers between devices with their start and end apart: 3, of which 2 were waited for; matrix products, arithmetic and copies ran while one was open for 56% of the time, Pallas kernels for 0%

commit v1 on v0

--- a/solution.py
+++ b/solution.py
@@ -111,9 +111,9 @@
     weight_total = lax.psum(weight_low, "leaf")
     def backward_part():
         output_gradient = contract_cols(shard_rows, out_weight).astype(jnp.bfloat16)
-        asking_heads = asking_matrix.reshape(tree_len, heads_local, HEAD_SIZE)
-        attended_heads = attended.reshape(tree_len, heads_local, HEAD_SIZE)
-        grad_heads = output_gradient.reshape(tree_len, heads_local, HEAD_SIZE)
+        asking_heads = jnp.transpose(asking_matrix.reshape(tree_len, heads_local, HEAD_SIZE), (1, 0, 2))
+        attended_heads = jnp.transpose(attended.reshape(tree_len, heads_local, HEAD_SIZE), (1, 0, 2))
+        grad_heads = jnp.transpose(output_gradient.reshape(tree_len, heads_local, HEAD_SIZE), (1, 0, 2))
         totals_heads = log_totals.reshape(heads_local, tree_len)
 
         def one_head(head_id, carry):
@@ -121,9 +121,9 @@
             kv_id = head_id // queries_per_group
             keys_all = lax.dynamic_index_in_dim(lookup_matrix, kv_id, axis=1, keepdims=False)
             values_all = lax.dynamic_index_in_dim(value_rows, kv_id, axis=1, keepdims=False)
-            query_all = lax.dynamic_index_in_dim(asking_heads, head_id, axis=1, keepdims=False)
-            grad_all = lax.dynamic_index_in_dim(grad_heads, head_id, axis=1, keepdims=False)
-            own_all = lax.dynamic_index_in_dim(attended_heads, head_id, axis=1, keepdims=False)
+            query_all = lax.dynamic_index_in_dim(asking_heads, head_id, axis=0, keepdims=False)
+            grad_all = lax.dynamic_index_in_dim(grad_heads, head_id, axis=0, keepdims=False)
+            own_all = lax.dynamic_index_in_dim(attended_heads, head_id, axis=0, keepdims=False)
             totals_all = lax.dynamic_index_in_dim(totals_heads, head_id, axis=0, keepdims=False)
             key_now = lax.dynamic_index_in_dim(key_acc, kv_id, axis=1, keepdims=False)
             value_now = lax.dynamic_index_in_dim(value_acc, kv_id, axis=1, keepdims=False)
@@ -164,7 +164,7 @@
             key_acc = lax.dynamic_update_index_in_dim(key_acc, key_now, kv_id, axis=1)
             value_acc = lax.dynamic_update_index_in_dim(value_acc, value_now, kv_id, axis=1)
             query_grad = lax.dynamic_update_index_in_dim(
-                query_grad, jnp.concatenate(query_blocks, axis=0), head_id, axis=1
+                query_grad, jnp.concatenate(query_blocks, axis=0), head_id, axis=0
             )
             return key_acc, value_acc, query_grad
 
@@ -175,10 +175,12 @@
             (
                 jnp.zeros((tree_len, kv_local, HEAD_SIZE), jnp.float32),
                 jnp.zeros((tree_len, kv_local, HEAD_SIZE), jnp.float32),
-                jnp.zeros((tree_len, heads_local, HEAD_SIZE), jnp.bfloat16),
+                jnp.zeros((heads_local, tree_len, HEAD_SIZE), jnp.bfloat16),
             ),
         )
-        query_grad = query_grad.reshape(tree_len, kv_local, queries_per_group, HEAD_SIZE)
+        query_grad = jnp.transpose(query_grad, (1, 0, 2)).reshape(
+            tree_len, kv_local, queries_per_group, HEAD_SIZE
+        )
         gradients = jnp.concatenate(
             [
                 query_grad,

time: 264 us -> 245 us (0.928)
  local copies, waits for them, and re-layouts: 71.9 us -> 54.9 us
  other arithmetic: 23.8 us -> 20.4 us
    dynamic_update_slice x10, local copies, waits for them, and re-layouts: 17.5 us -> 4.33 us  [one_head(): lax.dynamic_update_index_in_dim(query_grad, jnp.concatenate(query_blocks,...]
    while x3 -> x2, local copies, waits for them, and re-layouts: 4.16 us -> 0.27 us  [backward_part(): lax.fori_loop(0, heads_local, one_head, (jnp.zeros((tree_len, kv_local, H...]
    broadcast_in_dim x5, other arithmetic: 3.61 us -> 0.1 us  [one_head(): lax.dynamic_update_index_in_dim(query_grad, jnp.concatenate(query_blocks,...]
  transfers between devices with their start and end apart: 3 -> 3, of which waited for: 2 -> 2; matrix products, arithmetic and copies ran while one was open for 56% -> 53% of each run, Pallas kernels for 0% -> 0%
where the time goes in v1:
time: 245 us; the launch traced here: 243 us
  matrix products  74.1 us (30%)
  local copies, waits for them, and re-layouts  54.9 us (22%)
  waiting for transfers between devices  45.7 us (19%)
  blocking collectives  27 us (11%)
  other arithmetic  20.4 us (8%)
  between operations  14.3 us (6%)
  starting transfers between devices  5.97 us (2%)
    dot_general x21, matrix products, contract_cols(): lax.dot_general(left, right, (((1,), (1,)), ((), ())), preferred_element_...  32.8 us
    all_to_all x1, waiting for transfers between devices, local(): lax.all_to_all(query_key_value_rows, 'ctx', split_axis=1, concat_axis=0,...  32.5 us
    dot_general x21, matrix products, contract_rows(): lax.dot_general(left, right, (((0,), (0,)), ((), ())), preferred_element_...  29.1 us
    all_to_all x1, blocking collectives, local(): lax.all_to_all(gradients, 'ctx', split_axis=0, concat_axis=1, tiled=True)  27 us
    unnamed x23, local copies, waits for them, and re-layouts  16.2 us
    all_gather x1, waiting for transfers between devices, local(): shard_rows = lax.all_gather(cotangent, 'ctx', axis=0, tiled=True)  12.5 us
    reduce_sum x5, other arithmetic, one_head(): jnp.sum(grad_rows.astype(jnp.float32) * own_rows.astype(jnp.float32), axi...  5.98 us
    all_to_all x1, starting transfers between devices, local(): lax.all_to_all(query_key_value_rows, 'ctx', split_axis=1, concat_axis=0,...  5.93 us
  transfers between devices with their start and end apart: 3, of which 2 were waited for; matrix products, arithmetic and copies ran while one was open for 53% of the time, Pallas kernels for 0%

profile of v1, /device:TPU:1, one launch (start us, length us, event | category | flops | bytes accessed | tf_op | source)
XLA Modules:
  0.0 243.3 jit_solution(497299424066831932)
XLA Ops:
  7.9 3.9 %copy.56 = bf16[128,7168]{0,1:T(8,128)(2,1)} copy(bf16[128,7168]{1,0:T(8,128)(2,1)} %param.23) | data formatting | bytes 3670016 | tf_op args[0]
  11.8 5.9 %all-to-all-start = ((bf16[128,8,896]{0,2,1:T(8,128)(2,1)}), bf16[128,8,896]{0,2,1:T(8,128)(2,1)S(1)}, u32[]{:S(2)}, u32[]{:S(2)}) async-start(bf16[128,8,896]{0,2,1:T(8,128)(2,1)} %bitcast.311), calls=%async_computation | async-start | bytes 3670016 | tf_op jit(solution)/shard_map/all_to_all | solution.py:60
  17.7 2.2 while.53
  21.9 32.5 %all-to-all-done = bf16[128,8,896]{0,2,1:T(8,128)(2,1)S(1)} async-done(((bf16[128,8,896]{0,2,1:T(8,128)(2,1)}), bf16[128,8,896]{0,2,1:T(8,128)(2,1)S(1)}, u32[]{:S(2)}, u32[]{:S(2)}) %all-to-all-start) | async-done | bytes 1835040 | tf_op jit(solution)/shard_map/all_to_all | solution.py:60
  54.4 2.4 copy.57
  56.8 2.7 %reshape.561 = bf16[1024,1,7,128]{0,3,2,1:T(8,128)(2,1)S(1)} reshape(bf16[8,128,896]{1,0,2:T(8,128)(2,1)} %copy.57) | data formatting | bytes 3670016 | tf_op jit(solution)/shard_map/reshape | solution.py:64
  59.6 1.0 fusion.39
  60.6 1.1 exponential_reduce_fusion.1
  61.7 1.8 fusion.34
  63.5 2.2 exponential_reduce_fusion
  65.8 1.9 fusion.55
  67.7 3.9 %fusion.52 = bf16[512,1,5,128]{3,0,2,1:T(8,128)(2,1)S(1)} fusion(f32[1024,512,5]{1,0,2:T(8,128)S(1)} %get-tuple-element.661, f32[5,512]{1,0:T(8,128)S(1)} %log_add_fusion, f32[512]{0:T(512)S(1)} %get-tuple-element.659, pred[512,1024]{0,1:T(8,128)(4,1)S(1)} %fusion.45, bf16[1024,1,7,128]{0,3,2,1:T(8,128)(2,1)S(1)} %reshape.561), kind=kOutput, calls=%fused_computation.87 | convolution fusion | flops 681902080 | bytes 11945984 | tf_op jit(solution)/shard_map/gjts,sgd->tgjd/dot_general | solution.py:97
  71.7 1.5 copy.68
  73.2 12.5 %all-gather.2.cloned.1.call-done = bf16[1024,5120]{1,0:T(8,128)(2,1)} async-done(((bf16[128,5120]{1,0:T(8,128)(2,1)}), bf16[1024,5120]{1,0:T(8,128)(2,1)}) %all-gather.2.cloned.1.call-update) | async-done | bytes 10485776 | tf_op jit(solution)/shard_map/all_gather | solution.py:108
  85.6 11.7 %convolution_convert_fusion.3 = bf16[640,5120]{1,0:T(8,128)(2,1)} fusion(bf16[1024,640]{0,1:T(8,128)(2,1)} %bitcast.317, bf16[1024,5120]{1,0:T(8,128)(2,1)} %all-gather.2.cloned.1.call-done), kind=kOutput, calls=%fused_computation.69 | convolution fusion | flops 6714163200 | bytes 18350080 | tf_op jit(solution)/shard_map/dot_general | solution.py:47
  98.1 1.1 copy.80
  99.4 1.3 pad_maximum_fusion.2
  100.8 1.6 broadcast_in_dim.151
  102.3 2.4 broadcast_in_dim.155
  104.7 1.0 le.56
  105.8 1.2 le.55
  106.9 1.6 le.57
  108.5 84.4 %conditional.1 = (bf16[1024,896]{0,1:T(8,128)(2,1)S(1)}) conditional(s32[]{:T(128)} %convert_element_type.154, () %tuple.93, (bf16[1024,1,1,128]{3,0,2,1:T(8,128)(2,1)S(1)}, bf16[1024,1,1,128]{3,0,2,1:T(8,128)(2,1)S(1)}, bf16[1024,1,7,128]{0,3,2,1:T(8,128)(2,1)}, bf16[1024,5120]{1,0:T(8,128)(2,1)}, bf16[640,5120]{1,0:T(8,128)(2,1)}, ...), branch_computations={%region_7.8_spmd, %region_8.13_spmd} | conditional | flops 7731805184 | bytes 79870424 | solution.py:198
  108.5 3.2 %bitcast_and_fusion.1 = pred[512,512]{1,0:T(32,128)(4,1)} fusion(pred[64,8,4,128]{3,2,1,0:T(4,128)(4,1)S(1)} %bitcast.321, s32[512,512]{1,0:T(8,128)} %get-tuple-element.514, s32[512,512]{1,0:T(8,128)} %get-tuple-element.515, s32[512]{0:T(512)S(1)} %get-tuple-element.513), kind=kLoop, calls=%fused_computation.57 | loop fusion | flops 1310720 | bytes 2623488 | tf_op jit(solution)/shard_map/and | solution.py:37
  111.7 1.6 bitcast_and_fusion
  113.3 12.7 %convolution_convert_fusion.2 = bf16[1024,640]{0,1:T(8,128)(2,1)} fusion(bf16[1024,5120]{1,0:T(8,128)(2,1)} %get-tuple-element.517, bf16[640,5120]{1,0:T(8,128)(2,1)} %get-tuple-element.538), kind=kOutput, calls=%fused_computation.55 | convolution fusion | flops 6711541760 | bytes 18350080 | tf_op jit(solution)/shard_map/cond/branch_1_fun/dot_general | solution.py:53
  126.0 1.8 copy.52
  127.8 3.8 %copy.69 = bf16[1024,1,7,128]{3,0,2,1:T(8,128)(2,1)} copy(bf16[1024,1,7,128]{0,3,2,1:T(8,128)(2,1)} %get-tuple-element.599) | data formatting | bytes 3670016 | tf_op jit(solution)/shard_map
  131.6 2.6 %slice_bitcast_fusion = bf16[5,1024,128]{2,1,0:T(8,128)(2,1)} fusion(bf16[1024,1,7,128]{3,0,2,1:T(8,128)(2,1)} %copy.69), kind=kLoop, calls=%fused_computation.56 | loop fusion | bytes 2621440 | tf_op jit(solution)/shard_map/cond/branch_1_fun/transpose | solution.py:114
  134.2 56.7 %while.52 = (s32[]{:T(128)}, f32[1024,1,128]{2,0,1:T(8,128)S(1)}, f32[1024,1,128]{2,0,1:T(8,128)S(1)}, bf16[5,1024,128]{1,2,0:T(8,128)(2,1)}, bf16[5,1024,128]{2...) while((s32[]{:T(128)}, f32[1024,1,128]{2,0,1:T(8,128)S(1)}, ...), condition=%wide.region_12.12_spmd, body=%wide.region_9.11_spmd.sunk | while | flops 1014496256 | bytes 24809708 | solution.py:171
  134.4 1.2 fusion.127
  136.6 1.5 fusion.126
  138.7 1.3 fusion.129
  140.3 1.8 subtract_exponential_fusion.2
  143.0 1.4 fusion.130
  145.8 1.2 fusion.127
  147.9 1.4 fusion.126
  150.0 1.3 fusion.129
  151.6 1.8 subtract_exponential_fusion.2
  154.3 1.4 fusion.130
  157.1 1.2 fusion.127
  158.3 0.8 fusion.124
  159.2 1.4 fusion.126
  161.3 1.3 fusion.129
  162.9 1.8 subtract_exponential_fusion.2
  165.6 1.4 fusion.130
  168.4 1.2 fusion.127
  169.6 0.8 fusion.124
  170.5 1.4 fusion.126
  172.6 1.3 fusion.129
  174.2 1.8 subtract_exponential_fusion.2
  176.9 1.4 fusion.130
  179.7 1.2 fusion.127
  181.7 1.4 fusion.126
  183.9 1.3 fusion.129
  185.4 1.8 subtract_exponential_fusion.2
  188.2 1.4 fusion.130
  191.2 1.7 pad_maximum_fusion
  192.9 1.2 copy-done.3
  194.1 3.2 %copy.70 = bf16[1024,896]{1,0:T(8,128)(2,1)S(1)} copy(bf16[1024,896]{0,1:T(8,128)(2,1)} %copy-done.3) | data formatting | bytes 3670016 | tf_op jit(solution)/shard_map/cond | solution.py:198
  197.3 27.0 %all_to_all.35 = bf16[8,128,896]{2,1,0:T(8,128)(2,1)} all-to-all(bf16[8,128,896]{2,1,0:T(8,128)(2,1)S(1)} %bitcast.312), channel_id=1, replica_groups=mesh['leaf'=16,'ctx'=8] {'ctx'}, dimensions={0} | all-to-all | bytes 3670016 | tf_op jit(solution)/shard_map/all_to_all | solution.py:199
  224.3 3.2 %copy.71 = bf16[8,128,896]{1,2,0:T(8,128)(2,1)S(1)} copy(bf16[8,128,896]{2,1,0:T(8,128)(2,1)} %all_to_all.35) | data formatting | bytes 3670016 | tf_op jit(solution)/shard_map/all_to_all | solution.py:199
  227.4 2.9 %copy.72 = bf16[128,7168]{1,0:T(8,128)(2,1)} copy(bf16[128,7168]{0,1:T(8,128)(2,1)S(1)} %bitcast.313) | data formatting | bytes 3670016
  230.3 6.1 %copy.126 = bf16[640,5120]{1,0:T(8,128)(2,1)} copy(bf16[640,5120]{1,0:T(8,128)(2,1)} %all-reduce.2.cloned.1.call-done) | data formatting | bytes 13107200
  (138 shorter events, 25.3 us)
Async XLA Ops:
  7.2 78.5 %all-gather.2.cloned.1.call-start = ((), (), s32[]{:S(2)}) async-start(), calls=%async_computation.2 | async-start | bytes 11796480 | tf_op jit(solution)/shard_map/all_gather | solution.py:108
  11.8 6.0 %copy-start.10 = (s32[1,8]{1,0:T(1,128)S(1)}, s32[1,8]{1,0:T(1,128)}, u32[]{:S(2)}) copy-start(s32[1,8]{1,0:T(1,128)} %param.26) | copy-start | bytes 100
  11.8 10.1 %copy-start.9 = (s32[1024]{0:T(1024)S(1)}, s32[1024]{0:T(1024)}, u32[]{:S(2)}) copy-start(s32[1024]{0:T(1024)} %param.27) | copy-start | bytes 12292
  11.8 42.6 %all-to-all-start = ((bf16[128,8,896]{0,2,1:T(8,128)(2,1)}), bf16[128,8,896]{0,2,1:T(8,128)(2,1)S(1)}, u32[]{:S(2)}, u32[]{:S(2)}) async-start(bf16[128,8,896]{0,2,1:T(8,128)(2,1)} %bitcast.311), calls=%async_computation | async-start | bytes 3670016 | tf_op jit(solution)/shard_map/all_to_all | solution.py:60
  17.7 212.6 %all-reduce.2.cloned.1.call-start = ((), (), s32[]{:S(2)}) async-start(), calls=%async_computation.3 | async-start | bytes 13107200 | tf_op jit(solution)/shard_map/psum | solution.py:111
  20.6 0.6 copy-start.7
  59.6 37.8 %copy-start = (bf16[1024,1,7,128]{0,3,2,1:T(8,128)(2,1)}, bf16[1024,1,7,128]{0,3,2,1:T(8,128)(2,1)S(1)}, u32[]{:S(2)}) copy-start(bf16[1024,1,7,128]{0,3,2,1:T(8,128)(2,1)S(1)} %reshape.561) | copy-start | bytes 5505028
  61.7 4.1 %copy-start.5 = (f32[5,512]{1,0:T(8,128)}, f32[5,512]{1,0:T(8,128)S(1)}, u32[]{:S(2)}) copy-start(f32[5,512]{1,0:T(8,128)S(1)} %log_add_fusion.1) | copy-start | bytes 30724
  65.8 1.9 copy-start.6
  104.7 3.8 %copy-start.8 = (s32[512]{0:T(512)S(1)}, s32[512]{0:T(512)}, u32[]{:S(2)}) copy-start(s32[512]{0:T(512)} %copy-done.7) | copy-start | bytes 6148
  108.5 4.8 %copy-start.1 = (bf16[1024,1,5,128]{3,0,2,1:T(8,128)(2,1)}, bf16[1024,1,5,128]{3,0,2,1:T(8,128)(2,1)S(1)}, u32[]{:S(2)}) copy-start(bf16[1024,1,5,128]{3,0,2,1:T(8,128)(2,1)S(1)} %get-tuple-element.520) | copy-start | bytes 3932164 | tf_op jit(solution)/shard_map/cond
  108.5 3.2 %copy-start.4 = (pred[512,8,128]{2,1,0:T(8,128)(4,1)S(1)}, pred[512,8,128]{2,1,0:T(8,128)(4,1)}, u32[]{:S(2)}) copy-start(pred[512,8,128]{2,1,0:T(8,128)(4,1)} %get-tuple-element.521) | copy-start | bytes 1572868 | tf_op jit(solution)/shard_map/cond
  108.5 3.2 %copy-start.2 = (s32[512,1024]{1,0:T(8,128)S(1)}, s32[512,1024]{1,0:T(8,128)}, u32[]{:S(2)}) copy-start(s32[512,1024]{1,0:T(8,128)} %get-tuple-element.524) | copy-start | bytes 6291460 | tf_op jit(solution)/shard_map/cond
  192.9 1.2 copy-start.3
Sparse Core Ops, SparseCore 0:
  9.7 75.9 all-gather.1
  97.5 124.9 all-reduce.1

commit v2 on v1

--- a/solution.py
+++ b/solution.py
@@ -135,8 +135,9 @@
                 keys_now = keys_all[:closing_slot]
                 values_now = values_all[:closing_slot]
                 line_multiplier = softness_multiplier[opening_slot:closing_slot][:, None]
+                allowed_now = token_mask(reached, opening_slot, block_len, closing_slot)
                 attention_logits = jnp.where(
-                    masks[block_id], contract_cols(query_now, keys_now) * line_multiplier, -jnp.inf
+                    allowed_now, contract_cols(query_now, keys_now) * line_multiplier, -jnp.inf
                 )
                 attention_probabilities = jnp.exp(
                     attention_logits - totals_all[opening_slot:closing_slot][:, None]

time: 245 us -> 247 us (level)
  other arithmetic: 20.4 us -> 14.5 us
  local copies, waits for them, and re-layouts: 54.9 us -> 59.3 us
  matrix products: 74.1 us -> 76.9 us
    broadcast_in_dim x4 -> x20, local copies, waits for them, and re-layouts: 4.02 us -> 16.2 us  [token_mask(): expanded = jnp.repeat(jnp.repeat(block_part, BLK, axis=0), BLK, axis=1)]
    and x4 -> x2, other arithmetic: 5.76 us -> 1 us  [token_mask(): expanded & (jnp.logical_not(same_block) | (key_pos[None, :] <= query_pos[...]
    le x3 -> x0, local copies, waits for them, and re-layouts: 3.77 us -> none  [token_mask(): key_pos[None, :] <= query_pos[:, None]]
    slice x5, local copies, waits for them, and re-layouts: 4.1 us -> 0.41 us  [one_head(): totals_all[opening_slot:closing_slot][:, None]]
    dot_general x21, matrix products: 32.8 us -> 35.6 us  [contract_cols(): lax.dot_general(left, right, (((1,), (1,)), ((), ())), preferred_element_...]
    unnamed x23 -> x15, local copies, waits for them, and re-layouts: 16.2 us -> 15.5 us
  transfers between devices with their start and end apart: 3 -> 3, of which waited for: 2 -> 2; matrix products, arithmetic and copies ran while one was open for 53% -> 54% of each run, Pallas kernels for 0% -> 0%
where the time goes in v2:
time: 247 us; the launch traced here: 245 us
  matrix products  76.9 us (31%)
  local copies, waits for them, and re-layouts  59.3 us (24%)
  waiting for transfers between devices  46.3 us (19%)
  blocking collectives  27 us (11%)
  other arithmetic  14.5 us (6%)
  between operations  14.2 us (6%)
  starting transfers between devices  5.97 us (2%)
    dot_general x21, matrix products, contract_cols(): lax.dot_general(left, right, (((1,), (1,)), ((), ())), preferred_element_...  35.6 us
    all_to_all x1, waiting for transfers between devices, local(): lax.all_to_all(query_key_value_rows, 'ctx', split_axis=1, concat_axis=0,...  33.1 us
    dot_general x21, matrix products, contract_rows(): lax.dot_general(left, right, (((0,), (0,)), ((), ())), preferred_element_...  29.1 us
    all_to_all x1, blocking collectives, local(): lax.all_to_all(gradients, 'ctx', split_axis=0, concat_axis=1, tiled=True)  27 us
    broadcast_in_dim x20, local copies, waits for them, and re-layouts, token_mask(): expanded = jnp.repeat(jnp.repeat(block_part, BLK, axis=0), BLK, axis=1)  16.2 us
    unnamed x15, local copies, waits for them, and re-layouts  15.5 us
    all_gather x1, waiting for transfers between devices, local(): shard_rows = lax.all_gather(cotangent, 'ctx', axis=0, tiled=True)  12.5 us
    reduce_sum x5, other arithmetic, one_head(): jnp.sum(grad_rows.astype(jnp.float32) * own_rows.astype(jnp.float32), axi...  5.99 us
  transfers between devices with their start and end apart: 3, of which 2 were waited for; matrix products, arithmetic and copies ran while one was open for 54% of the time, Pallas kernels for 0%

profile of v2, /device:TPU:1, one launch (start us, length us, event | category | flops | bytes accessed | tf_op | source)
XLA Modules:
  0.0 245.2 jit_solution(3668216444367439921)
XLA Ops:
  7.9 3.9 %copy.53 = bf16[128,7168]{0,1:T(8,128)(2,1)} copy(bf16[128,7168]{1,0:T(8,128)(2,1)} %param.23) | data formatting | bytes 3670016 | tf_op args[0]
  11.8 5.9 %all-to-all-start = ((bf16[128,8,896]{0,2,1:T(8,128)(2,1)}), bf16[128,8,896]{0,2,1:T(8,128)(2,1)S(1)}, u32[]{:S(2)}, u32[]{:S(2)}) async-start(bf16[128,8,896]{0,2,1:T(8,128)(2,1)} %bitcast.333), calls=%async_computation | async-start | bytes 3670016 | tf_op jit(solution)/shard_map/all_to_all | solution.py:60
  17.7 2.2 while.56
  21.3 33.1 %all-to-all-done = bf16[128,8,896]{0,2,1:T(8,128)(2,1)S(1)} async-done(((bf16[128,8,896]{0,2,1:T(8,128)(2,1)}), bf16[128,8,896]{0,2,1:T(8,128)(2,1)S(1)}, u32[]{:S(2)}, u32[]{:S(2)}) %all-to-all-start) | async-done | bytes 1835040 | tf_op jit(solution)/shard_map/all_to_all | solution.py:60
  54.4 2.4 copy.54
  56.8 2.7 %reshape.671 = bf16[1024,1,7,128]{0,3,2,1:T(8,128)(2,1)S(1)} reshape(bf16[8,128,896]{1,0,2:T(8,128)(2,1)} %copy.54) | data formatting | bytes 3670016 | tf_op jit(solution)/shard_map/reshape | solution.py:64
  59.6 1.0 fusion.52
  60.6 1.1 exponential_reduce_fusion.1
  61.7 1.8 fusion.47
  63.5 2.2 exponential_reduce_fusion
  65.8 1.9 fusion.68
  67.7 3.7 %fusion.65 = bf16[512,1,5,128]{3,0,2,1:T(8,128)(2,1)S(1)} fusion(f32[1024,512,5]{1,0,2:T(8,128)S(1)} %get-tuple-element.614, f32[5,512]{1,0:T(8,128)S(1)} %log_add_fusion, f32[512]{0:T(512)S(1)} %get-tuple-element.612, pred[512,1024]{0,1:T(8,128)(4,1)S(1)} %fusion.58, bf16[1024,1,7,128]{0,3,2,1:T(8,128)(2,1)S(1)} %reshape.671), kind=kOutput, calls=%fused_computation.114 | convolution fusion | flops 681902080 | bytes 11945984 | tf_op jit(solution)/shard_map/gjts,sgd->tgjd/dot_general | solution.py:97
  71.5 1.7 copy.64
  73.1 12.5 %all-gather.2.cloned.1.call-done = bf16[1024,5120]{1,0:T(8,128)(2,1)} async-done(((bf16[128,5120]{1,0:T(8,128)(2,1)}), bf16[1024,5120]{1,0:T(8,128)(2,1)}) %all-gather.2.cloned.1.call-update) | async-done | bytes 10485776 | tf_op jit(solution)/shard_map/all_gather | solution.py:108
  85.6 11.7 %convolution_convert_fusion.3 = bf16[640,5120]{1,0:T(8,128)(2,1)} fusion(bf16[1024,640]{0,1:T(8,128)(2,1)} %bitcast.341, bf16[1024,5120]{1,0:T(8,128)(2,1)} %all-gather.2.cloned.1.call-done), kind=kOutput, calls=%fused_computation.96 | convolution fusion | flops 6714163200 | bytes 18350080 | tf_op jit(solution)/shard_map/dot_general | solution.py:47
  98.1 1.1 copy.74
  99.4 95.5 %conditional.1 = (bf16[1024,896]{0,1:T(8,128)(2,1)S(1)}) conditional(s32[]{:T(128)} %convert_element_type.164, () %tuple.98, (bf16[1024,1,1,128]{3,0,2,1:T(8,128)(2,1)S(1)}, bf16[1024,1,1,128]{3,0,2,1:T(8,128)(2,1)S(1)}, bf16[1024,1,7,128]{0,3,2,1:T(8,128)(2,1)}, bf16[1024,5120]{1,0:T(8,128)(2,1)}, bf16[640,5120]{1,0:T(8,128)(2,1)}, ...), branch_computations={%region_7.8_spmd, %region_8.13_spmd} | conditional | flops 7731826176 | bytes 64428576 | solution.py:199
  99.4 13.0 %convolution_convert_fusion.2 = bf16[1024,640]{0,1:T(8,128)(2,1)} fusion(bf16[1024,5120]{1,0:T(8,128)(2,1)} %get-tuple-element.499, bf16[640,5120]{1,0:T(8,128)(2,1)} %get-tuple-element.515), kind=kOutput, calls=%fused_computation.83 | convolution fusion | flops 6711541760 | bytes 18350080 | tf_op jit(solution)/shard_map/cond/branch_1_fun/dot_general | solution.py:53
  112.4 1.8 copy.49
  114.2 3.8 %copy.65 = bf16[1024,1,7,128]{3,0,2,1:T(8,128)(2,1)} copy(bf16[1024,1,7,128]{0,3,2,1:T(8,128)(2,1)} %get-tuple-element.560) | data formatting | bytes 3670016 | tf_op jit(solution)/shard_map
  118.1 2.5 %slice_bitcast_fusion = bf16[5,1024,128]{2,1,0:T(8,128)(2,1)} fusion(bf16[1024,1,7,128]{3,0,2,1:T(8,128)(2,1)} %copy.65), kind=kLoop, calls=%fused_computation.84 | loop fusion | bytes 2621440 | tf_op jit(solution)/shard_map/cond/branch_1_fun/transpose | solution.py:114
  120.6 72.3 %while.55 = (s32[]{:T(128)}, f32[1024,1,128]{2,0,1:T(8,128)S(1)}, f32[1024,1,128]{2,0,1:T(8,128)S(1)}, bf16[5,1024,128]{1,2,0:T(8,128)(2,1)}, pred[8,8]{1,0:T(8,...) while((s32[]{:T(128)}, f32[1024,1,128]{2,0,1:T(8,128)S(1)}, ...), condition=%wide.region_12.12_spmd, body=%wide.region_9.11_spmd.sunk | while | flops 1018449408 | bytes 25631092 | solution.py:172
  120.9 1.2 fusion.140
  122.3 1.6 broadcast_in_dim.294
  123.9 1.6 broadcast_in_dim.296
  125.6 1.5 fusion.139
  127.7 1.3 fusion.142
  129.3 2.3 subtract_exponential_fusion.2
  132.5 1.4 fusion.143
  135.3 1.2 fusion.140
  136.6 1.6 broadcast_in_dim.294
  138.2 1.6 broadcast_in_dim.296
  139.9 1.5 fusion.139
  142.1 1.3 fusion.142
  143.7 2.3 subtract_exponential_fusion.2
  146.9 1.4 fusion.143
  149.7 1.2 fusion.140
  151.0 1.6 broadcast_in_dim.294
  152.6 1.6 broadcast_in_dim.296
  154.3 1.5 fusion.139
  156.5 1.3 fusion.142
  158.1 2.3 subtract_exponential_fusion.2
  161.3 1.4 fusion.143
  164.1 1.2 fusion.140
  165.4 1.6 broadcast_in_dim.294
  167.0 1.6 broadcast_in_dim.296
  168.7 1.5 fusion.139
  170.9 1.3 fusion.142
  172.5 2.3 subtract_exponential_fusion.2
  175.7 1.4 fusion.143
  178.5 1.2 fusion.140
  179.9 1.6 broadcast_in_dim.294
  181.5 1.6 broadcast_in_dim.296
  183.2 1.5 fusion.139
  185.3 1.3 fusion.142
  186.9 2.3 subtract_exponential_fusion.2
  190.1 1.4 fusion.143
  193.2 1.8 pad_maximum_fusion
  195.0 1.2 copy-done.2
  196.2 3.1 %copy.66 = bf16[1024,896]{1,0:T(8,128)(2,1)S(1)} copy(bf16[1024,896]{0,1:T(8,128)(2,1)} %copy-done.2) | data formatting | bytes 3670016 | tf_op jit(solution)/shard_map/cond | solution.py:199
  199.2 27.0 %all_to_all.35 = bf16[8,128,896]{2,1,0:T(8,128)(2,1)} all-to-all(bf16[8,128,896]{2,1,0:T(8,128)(2,1)S(1)} %bitcast.334), channel_id=1, replica_groups=mesh['leaf'=16,'ctx'=8] {'ctx'}, dimensions={0} | all-to-all | bytes 3670016 | tf_op jit(solution)/shard_map/all_to_all | solution.py:200
  226.3 3.2 %copy.67 = bf16[8,128,896]{1,2,0:T(8,128)(2,1)S(1)} copy(bf16[8,128,896]{2,1,0:T(8,128)(2,1)} %all_to_all.35) | data formatting | bytes 3670016 | tf_op jit(solution)/shard_map/all_to_all | solution.py:200
  229.4 2.9 %copy.68 = bf16[128,7168]{1,0:T(8,128)(2,1)} copy(bf16[128,7168]{0,1:T(8,128)(2,1)S(1)} %bitcast.335) | data formatting | bytes 3670016
  232.3 6.1 %copy.121 = bf16[640,5120]{1,0:T(8,128)(2,1)} copy(bf16[640,5120]{1,0:T(8,128)(2,1)} %all-reduce.2.cloned.1.call-done) | data formatting | bytes 13107200
  (164 shorter events, 22.9 us)
Async XLA Ops:
  7.2 78.5 %all-gather.2.cloned.1.call-start = ((), (), s32[]{:S(2)}) async-start(), calls=%async_computation.2 | async-start | bytes 11796480 | tf_op jit(solution)/shard_map/all_gather | solution.py:108
  11.8 6.0 %copy-start.4 = (s32[1,8]{1,0:T(1,128)S(1)}, s32[1,8]{1,0:T(1,128)}, u32[]{:S(2)}) copy-start(s32[1,8]{1,0:T(1,128)} %param.26) | copy-start | bytes 100
  11.8 9.5 %copy-start.3 = (s32[1024]{0:T(1024)S(1)}, s32[1024]{0:T(1024)}, u32[]{:S(2)}) copy-start(s32[1024]{0:T(1024)} %param.27) | copy-start | bytes 12292
  11.8 42.6 %all-to-all-start = ((bf16[128,8,896]{0,2,1:T(8,128)(2,1)}), bf16[128,8,896]{0,2,1:T(8,128)(2,1)S(1)}, u32[]{:S(2)}, u32[]{:S(2)}) async-start(bf16[128,8,896]{0,2,1:T(8,128)(2,1)} %bitcast.333), calls=%async_computation | async-start | bytes 3670016 | tf_op jit(solution)/shard_map/all_to_all | solution.py:60
  17.7 214.6 %all-reduce.2.cloned.1.call-start = ((), (), s32[]{:S(2)}) async-start(), calls=%async_computation.3 | async-start | bytes 13107200 | tf_op jit(solution)/shard_map/psum | solution.py:111
  59.6 37.8 %copy-start = (bf16[1024,1,7,128]{0,3,2,1:T(8,128)(2,1)}, bf16[1024,1,7,128]{0,3,2,1:T(8,128)(2,1)S(1)}, u32[]{:S(2)}) copy-start(bf16[1024,1,7,128]{0,3,2,1:T(8,128)(2,1)S(1)} %reshape.671) | copy-start | bytes 5505028
  99.4 13.0 %copy-start.1 = (bf16[1024,1,5,128]{3,0,2,1:T(8,128)(2,1)}, bf16[1024,1,5,128]{3,0,2,1:T(8,128)(2,1)S(1)}, u32[]{:S(2)}) copy-start(bf16[1024,1,5,128]{3,0,2,1:T(8,128)(2,1)S(1)} %get-tuple-element.502) | copy-start | bytes 3932164 | tf_op jit(solution)/shard_map/cond
  194.9 1.2 copy-start.2
Sparse Core Ops, SparseCore 0:
  9.7 75.9 all-gather.1
  97.5 124.9 all-reduce.1

commit v3 on v1

--- a/solution.py
+++ b/solution.py
@@ -107,7 +107,7 @@
     flat_out = attended.reshape(tree_len, heads_local * HEAD_SIZE)
     shard_rows = lax.all_gather(cotangent, "ctx", axis=0, tiled=True)
     weight_low = contract_rows(flat_out, shard_rows).astype(jnp.bfloat16)
-    weight_low, shard_rows = lax.optimization_barrier((weight_low, shard_rows))
+    weight_low, shard_rows, masks = lax.optimization_barrier((weight_low, shard_rows, masks))
     weight_total = lax.psum(weight_low, "leaf")
     def backward_part():
         output_gradient = contract_cols(shard_rows, out_weight).astype(jnp.bfloat16)

time: 245 us -> 242 us (0.988)
  matrix products: 74.1 us -> 90.5 us
  local copies, waits for them, and re-layouts: 54.9 us -> 46.7 us
  waiting for transfers between devices: 45.7 us -> 39.1 us
  other arithmetic: 20.4 us -> 16.1 us
    dot_general x21, matrix products: 29.1 us -> 38.2 us  [contract_rows(): lax.dot_general(left, right, (((0,), (0,)), ((), ())), preferred_element_...]
    dot_general x21, matrix products: 32.8 us -> 40.2 us  [contract_cols(): lax.dot_general(left, right, (((1,), (1,)), ((), ())), preferred_element_...]
    all_to_all x1, waiting for transfers between devices: 32.5 us -> 27.9 us  [local(): lax.all_to_all(query_key_value_rows, 'ctx', split_axis=1, concat_axis=0,...]
    and x4 -> x2, other arithmetic: 5.76 us -> 1.18 us  [token_mask(): expanded & (jnp.logical_not(same_block) | (key_pos[None, :] <= query_pos[...]
    le x3 -> x0, local copies, waits for them, and re-layouts: 3.77 us -> none  [token_mask(): key_pos[None, :] <= query_pos[:, None]]
    slice x5, local copies, waits for them, and re-layouts: 4.1 us -> 0.41 us  [one_head(): totals_all[opening_slot:closing_slot][:, None]]
    unnamed x23 -> x13, local copies, waits for them, and re-layouts: 16.2 us -> 14.4 us
  transfers between devices with their start and end apart: 3 -> 3, of which waited for: 2 -> 2; matrix products, arithmetic and copies ran while one was open for 53% -> 56% of each run, Pallas kernels for 0% -> 0%
where the time goes in v3:
time: 242 us; the launch traced here: 240 us
  matrix products  90.5 us (37%)
  local copies, waits for them, and re-layouts  46.7 us (19%)
  waiting for transfers between devices  39.1 us (16%)
  blocking collectives  27.1 us (11%)
  other arithmetic  16.1 us (7%)
  between operations  14.3 us (6%)
  starting transfers between devices  5.97 us (2%)
    dot_general x21, matrix products, contract_cols(): lax.dot_general(left, right, (((1,), (1,)), ((), ())), preferred_element_...  40.2 us
    dot_general x21, matrix products, contract_rows(): lax.dot_general(left, right, (((0,), (0,)), ((), ())), preferred_element_...  38.2 us
    all_to_all x1, waiting for transfers between devices, local(): lax.all_to_all(query_key_value_rows, 'ctx', split_axis=1, concat_axis=0,...  27.9 us
    all_to_all x1, blocking collectives, local(): lax.all_to_all(gradients, 'ctx', split_axis=0, concat_axis=1, tiled=True)  27.1 us
    unnamed x13, local copies, waits for them, and re-layouts  14.4 us
    all_gather x1, waiting for transfers between devices, local(): shard_rows = lax.all_gather(cotangent, 'ctx', axis=0, tiled=True)  10.5 us
    reduce_sum x5, other arithmetic, one_head(): jnp.sum(grad_rows.astype(jnp.float32) * own_rows.astype(jnp.float32), axi...  6.61 us
    all_to_all x1, starting transfers between devices, local(): lax.all_to_all(query_key_value_rows, 'ctx', split_axis=1, concat_axis=0,...  5.93 us
  transfers between devices with their start and end apart: 3, of which 2 were waited for; matrix products, arithmetic and copies ran while one was open for 56% of the time, Pallas kernels for 0%

profile of v3, /device:TPU:1, one launch (start us, length us, event | category | flops | bytes accessed | tf_op | source)
XLA Modules:
  0.0 240.2 jit_solution(18008208691982613157)
XLA Ops:
  7.9 3.9 %copy.56 = bf16[128,7168]{0,1:T(8,128)(2,1)} copy(bf16[128,7168]{1,0:T(8,128)(2,1)} %param.23) | data formatting | bytes 3670016 | tf_op args[0]
  11.8 5.9 %all-to-all-start = ((bf16[128,8,896]{0,2,1:T(8,128)(2,1)}), bf16[128,8,896]{0,2,1:T(8,128)(2,1)S(1)}, u32[]{:S(2)}, u32[]{:S(2)}) async-start(bf16[128,8,896]{0,2,1:T(8,128)(2,1)} %bitcast.306), calls=%async_computation | async-start | bytes 3670016 | tf_op jit(solution)/shard_map/all_to_all | solution.py:60
  17.7 2.2 while.53
  20.0 1.6 broadcast_in_dim.151
  22.4 1.6 broadcast_in_dim.155
  24.9 1.6 copy.65
  26.5 27.9 %all-to-all-done = bf16[128,8,896]{0,2,1:T(8,128)(2,1)S(1)} async-done(((bf16[128,8,896]{0,2,1:T(8,128)(2,1)}), bf16[128,8,896]{0,2,1:T(8,128)(2,1)S(1)}, u32[]{:S(2)}, u32[]{:S(2)}) %all-to-all-start) | async-done | bytes 1835040 | tf_op jit(solution)/shard_map/all_to_all | solution.py:60
  54.4 2.4 %copy.57 = bf16[8,128,896]{1,0,2:T(8,128)(2,1)} copy(bf16[8,128,896]{1,2,0:T(8,128)(2,1)S(1)} %bitcast.305) | data formatting | bytes 3670016 | tf_op jit(solution)/shard_map/all_to_all | solution.py:60
  56.8 2.9 %reshape.555 = bf16[1024,1,7,128]{0,3,2,1:T(8,128)(2,1)S(1)} reshape(bf16[8,128,896]{1,0,2:T(8,128)(2,1)} %copy.57) | data formatting | bytes 3670016 | tf_op jit(solution)/shard_map/reshape | solution.py:64
  61.9 1.8 fusion.34
  63.7 2.2 exponential_reduce_fusion
  65.9 1.9 fusion.55
  67.9 3.7 %fusion.52 = bf16[512,1,5,128]{3,0,2,1:T(8,128)(2,1)S(1)} fusion(f32[1024,512,5]{1,0,2:T(8,128)S(1)} %get-tuple-element.605, f32[5,512]{1,0:T(8,128)S(1)} %log_add_fusion, f32[512]{0:T(512)S(1)} %get-tuple-element.603, pred[512,1024]{0,1:T(8,128)(4,1)S(1)} %copy-done.1, bf16[1024,1,7,128]{0,3,2,1:T(8,128)(2,1)S(1)} %reshape.555), kind=kOutput, calls=%fused_computation.85 | convolution fusion | flops 681902080 | bytes 11945984 | tf_op jit(solution)/shard_map/gjts,sgd->tgjd/dot_general | solution.py:97
  72.7 2.4 %copy.68 = bf16[1024,1,5,128]{0,3,2,1:T(8,128)(2,1)} copy(bf16[1024,1,5,128]{3,0,2,1:T(8,128)(2,1)} %pad_maximum_fusion.1) | data formatting | bytes 2621440 | tf_op jit(solution)/shard_map/concatenate | solution.py:105
  75.2 10.5 %all-gather.2.cloned.1.call-done = bf16[1024,5120]{1,0:T(8,128)(2,1)} async-done(((bf16[128,5120]{1,0:T(8,128)(2,1)}), bf16[1024,5120]{1,0:T(8,128)(2,1)}) %all-gather.2.cloned.1.call-update) | async-done | bytes 10485776 | tf_op jit(solution)/shard_map/all_gather | solution.py:108
  85.6 11.7 %convolution_convert_fusion.3 = bf16[640,5120]{1,0:T(8,128)(2,1)} fusion(bf16[1024,640]{0,1:T(8,128)(2,1)} %bitcast.312, bf16[1024,5120]{1,0:T(8,128)(2,1)} %all-gather.2.cloned.1.call-done), kind=kOutput, calls=%fused_computation.67 | convolution fusion | flops 6714163200 | bytes 18350080 | tf_op jit(solution)/shard_map/dot_general | solution.py:47
  97.8 91.9 %conditional.1 = (bf16[1024,896]{0,1:T(8,128)(2,1)S(1)}) conditional(s32[]{:T(128)} %convert_element_type.154, () %tuple.93, (bf16[1024,1,1,128]{3,0,2,1:T(8,128)(2,1)S(1)}, bf16[1024,1,1,128]{3,0,2,1:T(8,128)(2,1)S(1)}, bf16[1024,1,7,128]{0,3,2,1:T(8,128)(2,1)S(1)}, bf16[1024,5120]{1,0:T(8,128)(2,1)}, bf16[640,5120]{1,0:T(8,128)(2,1)}, ...), branch_computations={%region_7.8_spmd, %region_8.13_spmd} | conditional | flops 7727873024 | bytes 58364292 | solution.py:198
  97.8 12.7 %convolution_convert_fusion.2 = bf16[1024,640]{0,1:T(8,128)(2,1)} fusion(bf16[1024,5120]{1,0:T(8,128)(2,1)} %get-tuple-element.482, bf16[640,5120]{1,0:T(8,128)(2,1)} %get-tuple-element.503), kind=kOutput, calls=%fused_computation.54 | convolution fusion | flops 6711541760 | bytes 18350080 | tf_op jit(solution)/shard_map/cond/branch_1_fun/dot_general | solution.py:53
  110.4 2.4 %copy.52 = bf16[1024,5,128]{2,0,1:T(8,128)(2,1)} copy(bf16[1024,5,128]{0,2,1:T(8,128)(2,1)} %bitcast.313) | data formatting | bytes 2621440 | tf_op jit(solution)/shard_map/cond/branch_1_fun/reshape | solution.py:116
  112.9 2.4 %copy.69 = bf16[1024,1,7,128]{3,0,2,1:T(8,128)(2,1)} copy(bf16[1024,1,7,128]{0,3,2,1:T(8,128)(2,1)S(1)} %get-tuple-element.550) | data formatting | bytes 3670016 | tf_op jit(solution)/shard_map
  115.3 2.5 %slice_bitcast_fusion = bf16[5,1024,128]{2,1,0:T(8,128)(2,1)} fusion(bf16[1024,1,7,128]{3,0,2,1:T(8,128)(2,1)} %copy.69), kind=kLoop, calls=%fused_computation.55 | loop fusion | bytes 2621440 | tf_op jit(solution)/shard_map/cond/branch_1_fun/transpose | solution.py:114
  117.9 70.0 %while.52 = (s32[]{:T(128)}, f32[1024,1,128]{2,0,1:T(8,128)S(1)}, f32[1024,1,128]{2,0,1:T(8,128)S(1)}, bf16[5,1024,128]{1,2,0:T(8,128)(2,1)}, bf16[5,1024,128]{2...) while((s32[]{:T(128)}, f32[1024,1,128]{2,0,1:T(8,128)S(1)}, ...), condition=%wide.region_12.12_spmd, body=%wide.region_9.11_spmd.sunk | while | flops 1014496256 | bytes 24809708 | solution.py:171
  117.9 1.3 fusion.127
  119.4 1.3 fusion.126
  120.7 1.3 fusion.131
  123.2 1.3 fusion.129
  124.8 1.6 subtract_exponential_fusion.2
  126.3 1.4 fusion.132
  127.7 1.4 multiply_convert_fusion.2
  129.1 1.4 fusion.130
  131.9 1.4 fusion.127
  133.4 1.3 fusion.126
  134.7 1.3 fusion.131
  138.8 1.6 subtract_exponential_fusion.2
  140.3 1.4 fusion.132
  141.7 1.4 multiply_convert_fusion.2
  143.1 1.4 fusion.130
  145.9 1.3 fusion.127
  147.3 1.3 fusion.126
  148.7 1.3 fusion.131
  151.2 1.3 fusion.129
  152.7 1.6 subtract_exponential_fusion.2
  154.3 1.4 fusion.132
  155.7 1.4 multiply_convert_fusion.2
  157.1 1.4 fusion.130
  159.9 1.3 fusion.127
  161.3 1.3 fusion.126
  166.7 1.6 subtract_exponential_fusion.2
  168.3 1.4 fusion.132
  169.7 1.4 multiply_convert_fusion.2
  171.1 1.4 fusion.130
  173.8 1.3 fusion.127
  175.3 1.3 fusion.126
  179.2 1.3 fusion.129
  180.7 1.6 subtract_exponential_fusion.2
  182.3 1.4 fusion.132
  183.7 1.4 multiply_convert_fusion.2
  185.1 1.4 fusion.130
  188.1 1.5 pad_maximum_fusion
  190.9 3.2 %copy.70 = bf16[1024,896]{1,0:T(8,128)(2,1)S(1)} copy(bf16[1024,896]{0,1:T(8,128)(2,1)} %copy-done) | data formatting | bytes 3670016 | tf_op jit(solution)/shard_map/cond | solution.py:198
  194.1 27.1 %all_to_all.35 = bf16[8,128,896]{2,1,0:T(8,128)(2,1)} all-to-all(bf16[8,128,896]{2,1,0:T(8,128)(2,1)S(1)} %bitcast.307), channel_id=1, replica_groups=mesh['leaf'=16,'ctx'=8] {'ctx'}, dimensions={0} | all-to-all | bytes 3670016 | tf_op jit(solution)/shard_map/all_to_all | solution.py:199
  221.2 3.2 %copy.71 = bf16[8,128,896]{1,2,0:T(8,128)(2,1)S(1)} copy(bf16[8,128,896]{2,1,0:T(8,128)(2,1)} %all_to_all.35) | data formatting | bytes 3670016 | tf_op jit(solution)/shard_map/all_to_all | solution.py:199
  224.4 2.9 %copy.72 = bf16[128,7168]{1,0:T(8,128)(2,1)} copy(bf16[128,7168]{0,1:T(8,128)(2,1)S(1)} %bitcast.308) | data formatting | bytes 3670016
  227.3 6.1 %copy.122 = bf16[640,5120]{1,0:T(8,128)(2,1)} copy(bf16[640,5120]{1,0:T(8,128)(2,1)} %all-reduce.2.cloned.1.call-done) | data formatting | bytes 13107200
  (119 shorter events, 29.9 us)
Async XLA Ops:
  7.2 78.5 %all-gather.2.cloned.1.call-start = ((), (), s32[]{:S(2)}) async-start(), calls=%async_computation.2 | async-start | bytes 11796480 | tf_op jit(solution)/shard_map/all_gather | solution.py:108
  11.8 6.0 %copy-start.3 = (s32[1,8]{1,0:T(1,128)S(1)}, s32[1,8]{1,0:T(1,128)}, u32[]{:S(2)}) copy-start(s32[1,8]{1,0:T(1,128)} %param.26) | copy-start | bytes 100
  11.8 42.6 %all-to-all-start = ((bf16[128,8,896]{0,2,1:T(8,128)(2,1)}), bf16[128,8,896]{0,2,1:T(8,128)(2,1)S(1)}, u32[]{:S(2)}, u32[]{:S(2)}) async-start(bf16[128,8,896]{0,2,1:T(8,128)(2,1)} %bitcast.306), calls=%async_computation | async-start | bytes 3670016 | tf_op jit(solution)/shard_map/all_to_all | solution.py:60
  17.7 209.5 %all-reduce.2.cloned.1.call-start = ((), (), s32[]{:S(2)}) async-start(), calls=%async_computation.3 | async-start | bytes 13107200 | tf_op jit(solution)/shard_map/psum | solution.py:111
  20.0 6.5 %copy-start.2 = (s32[1024]{0:T(1024)S(1)}, s32[1024]{0:T(1024)}, u32[]{:S(2)}) copy-start(s32[1024]{0:T(1024)} %param.27) | copy-start | bytes 12292
  60.8 1.1 copy-start.1
  189.7 1.2 copy-start
Sparse Core Ops, SparseCore 0:
  9.7 75.9 all-gather.1
  97.5 124.9 all-reduce.1

commit v4 on v3

--- a/solution.py
+++ b/solution.py
@@ -107,12 +107,16 @@
     flat_out = attended.reshape(tree_len, heads_local * HEAD_SIZE)
     shard_rows = lax.all_gather(cotangent, "ctx", axis=0, tiled=True)
     weight_low = contract_rows(flat_out, shard_rows).astype(jnp.bfloat16)
-    weight_low, shard_rows, masks = lax.optimization_barrier((weight_low, shard_rows, masks))
+    asking_heads = jnp.transpose(asking_matrix.reshape(tree_len, heads_local, HEAD_SIZE), (1, 0, 2))
+    attended_heads = jnp.transpose(attended.reshape(tree_len, heads_local, HEAD_SIZE), (1, 0, 2))
+    (
+        weight_low, shard_rows, masks, asking_heads, attended_heads, lookup_matrix, value_rows, log_totals
+    ) = lax.optimization_barrier(
+        (weight_low, shard_rows, masks, asking_heads, attended_heads, lookup_matrix, value_rows, log_totals)
+    )
     weight_total = lax.psum(weight_low, "leaf")
     def backward_part():
         output_gradient = contract_cols(shard_rows, out_weight).astype(jnp.bfloat16)
-        asking_heads = jnp.transpose(asking_matrix.reshape(tree_len, heads_local, HEAD_SIZE), (1, 0, 2))
-        attended_heads = jnp.transpose(attended.reshape(tree_len, heads_local, HEAD_SIZE), (1, 0, 2))
         grad_heads = jnp.transpose(output_gradient.reshape(tree_len, heads_local, HEAD_SIZE), (1, 0, 2))
         totals_heads = log_totals.reshape(heads_local, tree_len)
 

time: 242 us -> 237 us (0.979)
  local copies, waits for them, and re-layouts: 46.7 us -> 43.5 us
    all_gather x1, waiting for transfers between devices: 10.5 us -> 6.48 us  [local(): shard_rows = lax.all_gather(cotangent, 'ctx', axis=0, tiled=True)]
    another operation x3 -> x2, local copies, waits for them, and re-layouts: 2.51 us -> 0.07 us
  transfers between devices with their start and end apart: 3 -> 3, of which waited for: 2 -> 3; matrix products, arithmetic and copies ran while one was open for 56% -> 56% of each run, Pallas kernels for 0% -> 0%
where the time goes in v4:
time: 237 us; the launch traced here: 235 us
  matrix products  89.8 us (38%)
  local copies, waits for them, and re-layouts  43.5 us (18%)
  waiting for transfers between devices  37.4 us (16%)
  blocking collectives  27 us (11%)
  other arithmetic  16.8 us (7%)
  between operations  14.2 us (6%)
  starting transfers between devices  5.97 us (3%)
    dot_general x21, matrix products, contract_cols(): lax.dot_general(left, right, (((1,), (1,)), ((), ())), preferred_element_...  39.5 us
    dot_general x21, matrix products, contract_rows(): lax.dot_general(left, right, (((0,), (0,)), ((), ())), preferred_element_...  38.2 us
    all_to_all x1, waiting for transfers between devices, local(): lax.all_to_all(query_key_value_rows, 'ctx', split_axis=1, concat_axis=0,...  27.9 us
    all_to_all x1, blocking collectives, local(): lax.all_to_all(gradients, 'ctx', split_axis=0, concat_axis=1, tiled=True)  27 us
    unnamed x13, local copies, waits for them, and re-layouts  15.4 us
    reduce_sum x5, other arithmetic, one_head(): jnp.sum(grad_rows.astype(jnp.float32) * own_rows.astype(jnp.float32), axi...  6.59 us
    all_gather x1, waiting for transfers between devices, local(): shard_rows = lax.all_gather(cotangent, 'ctx', axis=0, tiled=True)  6.48 us
    all_to_all x1, starting transfers between devices, local(): lax.all_to_all(query_key_value_rows, 'ctx', split_axis=1, concat_axis=0,...  5.93 us
  transfers between devices with their start and end apart: 3, of which 3 were waited for; matrix products, arithmetic and copies ran while one was open for 56% of the time, Pallas kernels for 0%

profile of v4, /device:TPU:1, one launch (start us, length us, event | category | flops | bytes accessed | tf_op | source)
XLA Modules:
  0.0 235.3 jit_solution(3943057925726047068)
XLA Ops:
  7.9 3.9 %copy.59 = bf16[128,7168]{0,1:T(8,128)(2,1)} copy(bf16[128,7168]{1,0:T(8,128)(2,1)} %param.23) | data formatting | bytes 3670016 | tf_op args[0]
  11.8 5.9 %all-to-all-start = ((bf16[128,8,896]{0,2,1:T(8,128)(2,1)}), bf16[128,8,896]{0,2,1:T(8,128)(2,1)S(1)}, u32[]{:S(2)}, u32[]{:S(2)}) async-start(bf16[128,8,896]{0,2,1:T(8,128)(2,1)} %bitcast.310), calls=%async_computation | async-start | bytes 3670016 | tf_op jit(solution)/shard_map/all_to_all | solution.py:60
  17.7 2.2 while.53
  20.0 1.6 broadcast_in_dim.151
  22.4 1.6 broadcast_in_dim.155
  24.9 1.6 copy.65
  26.5 27.9 %all-to-all-done = bf16[128,8,896]{0,2,1:T(8,128)(2,1)S(1)} async-done(((bf16[128,8,896]{0,2,1:T(8,128)(2,1)}), bf16[128,8,896]{0,2,1:T(8,128)(2,1)S(1)}, u32[]{:S(2)}, u32[]{:S(2)}) %all-to-all-start) | async-done | bytes 1835040 | tf_op jit(solution)/shard_map/all_to_all | solution.py:60
  54.4 2.4 %copy.60 = bf16[8,128,896]{1,0,2:T(8,128)(2,1)} copy(bf16[8,128,896]{1,2,0:T(8,128)(2,1)S(1)} %bitcast.309) | data formatting | bytes 3670016 | tf_op jit(solution)/shard_map/all_to_all | solution.py:60
  56.8 2.9 %reshape.557 = bf16[1024,1,7,128]{0,3,2,1:T(8,128)(2,1)S(1)} reshape(bf16[8,128,896]{1,0,2:T(8,128)(2,1)} %copy.60) | data formatting | bytes 3670016 | tf_op jit(solution)/shard_map/reshape | solution.py:64
  64.0 1.8 fusion.34
  65.8 2.2 exponential_reduce_fusion
  68.0 1.9 fusion.55
  69.9 3.7 %fusion.52 = bf16[512,1,5,128]{3,0,2,1:T(8,128)(2,1)S(1)} fusion(f32[1024,512,5]{1,0,2:T(8,128)S(1)} %get-tuple-element.624, f32[5,512]{1,0:T(8,128)S(1)} %log_add_fusion, f32[512]{0:T(512)S(1)} %get-tuple-element.622, pred[512,1024]{0,1:T(8,128)(4,1)S(1)} %copy-done.1, bf16[1024,1,7,128]{0,3,2,1:T(8,128)(2,1)S(1)} %reshape.557), kind=kOutput, calls=%fused_computation.85 | convolution fusion | flops 681902080 | bytes 11945984 | tf_op jit(solution)/shard_map/gjts,sgd->tgjd/dot_general | solution.py:97
  73.6 1.9 fusion.77
  75.5 2.5 %copy.70 = bf16[1024,1,5,128]{0,3,2,1:T(8,128)(2,1)} copy(bf16[1024,1,5,128]{3,0,2,1:T(8,128)(2,1)} %get-tuple-element.620) | data formatting | bytes 2621440 | tf_op jit(solution)/shard_map/concatenate | solution.py:105
  79.1 6.5 %all-gather.2.cloned.1.call-done = bf16[1024,5120]{1,0:T(8,128)(2,1)} async-done(((bf16[128,5120]{1,0:T(8,128)(2,1)}), bf16[1024,5120]{1,0:T(8,128)(2,1)}) %all-gather.2.cloned.1.call-update) | async-done | bytes 10485776 | tf_op jit(solution)/shard_map/all_gather | solution.py:108
  85.6 11.7 %convolution_convert_fusion.3 = bf16[640,5120]{1,0:T(8,128)(2,1)} fusion(bf16[1024,640]{0,1:T(8,128)(2,1)} %bitcast.316, bf16[1024,5120]{1,0:T(8,128)(2,1)} %all-gather.2.cloned.1.call-done), kind=kOutput, calls=%fused_computation.66 | convolution fusion | flops 6714163200 | bytes 18350080 | tf_op jit(solution)/shard_map/dot_general | solution.py:47
  97.4 85.4 %conditional.1 = (bf16[1024,896]{0,1:T(8,128)(2,1)S(1)}) conditional(s32[]{:T(128)} %convert_element_type.154, () %tuple.93, (bf16[1024,5120]{1,0:T(8,128)(2,1)}, bf16[640,5120]{1,0:T(8,128)(2,1)}, f32[1,5,1024]{2,1,0:T(8,128)S(1)}, bf16[5,1024,128]{1,2,0:T(8,128)(2,1)}, bf16[1024,1,128]{2,0,1:T(8,128)(2,1)S(1)}, /*index=5*/f32[1024]{0:T(1024)S(1)}, ...), branch_computations={%region_7.8_spmd, %region_8.13_spmd} | conditional | flops 7727873024 | bytes 52072836 | solution.py:202
  97.4 11.6 %convolution_convert_fusion.2 = bf16[1024,640]{0,1:T(8,128)(2,1)S(1)} fusion(bf16[1024,5120]{1,0:T(8,128)(2,1)} %get-tuple-element.479, bf16[640,5120]{1,0:T(8,128)(2,1)} %get-tuple-element.510), kind=kOutput, calls=%fused_computation.54 | convolution fusion | flops 6711541760 | bytes 18350080 | tf_op jit(solution)/shard_map/cond/branch_1_fun/dot_general | solution.py:53
  109.0 1.4 copy.54
  110.5 70.4 %while.52 = (s32[]{:T(128)}, f32[1024,1,128]{2,0,1:T(8,128)S(1)}, f32[1024,1,128]{2,0,1:T(8,128)S(1)}, bf16[5,1024,128]{1,2,0:T(8,128)(2,1)}, bf16[5,1024,128]{1...) while((s32[]{:T(128)}, f32[1024,1,128]{2,0,1:T(8,128)S(1)}, ...), condition=%wide.region_12.12_spmd, body=%wide.region_9.11_spmd.sunk | while | flops 1014496256 | bytes 24809708 | solution.py:175
  110.5 1.3 fusion.128
  112.0 1.4 fusion.127
  117.5 1.6 subtract_exponential_fusion.2
  119.1 1.4 fusion.133
  120.5 1.4 multiply_convert_fusion.2
  121.9 1.4 fusion.131
  124.6 1.3 fusion.128
  126.1 1.4 fusion.127
  127.5 1.3 fusion.132
  130.0 1.3 fusion.130
  131.5 1.6 subtract_exponential_fusion.2
  133.2 1.4 fusion.133
  134.6 1.4 multiply_convert_fusion.2
  136.0 1.4 fusion.131
  138.7 1.3 fusion.128
  140.2 1.3 fusion.127
  141.5 1.3 fusion.132
  144.0 1.3 fusion.130
  145.6 1.6 subtract_exponential_fusion.2
  147.2 1.4 fusion.133
  148.6 1.4 multiply_convert_fusion.2
  150.0 1.4 fusion.131
  152.8 1.3 fusion.128
  154.3 1.4 fusion.127
  155.6 1.3 fusion.132
  159.7 1.6 subtract_exponential_fusion.2
  161.3 1.4 fusion.133
  162.7 1.4 multiply_convert_fusion.2
  164.1 1.4 fusion.131
  166.8 1.3 fusion.128
  168.3 1.4 fusion.127
  169.7 1.3 fusion.132
  173.8 1.6 subtract_exponential_fusion.2
  175.4 1.4 fusion.133
  176.8 1.4 multiply_convert_fusion.2
  178.2 1.4 fusion.131
  181.2 1.5 pad_maximum_fusion
  184.0 3.1 %copy.72 = bf16[1024,896]{1,0:T(8,128)(2,1)S(1)} copy(bf16[1024,896]{0,1:T(8,128)(2,1)} %copy-done) | data formatting | bytes 3670016 | tf_op jit(solution)/shard_map/cond | solution.py:202
  187.0 27.0 %all_to_all.35 = bf16[8,128,896]{2,1,0:T(8,128)(2,1)} all-to-all(bf16[8,128,896]{2,1,0:T(8,128)(2,1)S(1)} %bitcast.311), channel_id=1, replica_groups=mesh['leaf'=16,'ctx'=8] {'ctx'}, dimensions={0} | all-to-all | bytes 3670016 | tf_op jit(solution)/shard_map/all_to_all | solution.py:203
  214.0 3.2 %copy.73 = bf16[8,128,896]{1,2,0:T(8,128)(2,1)S(1)} copy(bf16[8,128,896]{2,1,0:T(8,128)(2,1)} %all_to_all.35) | data formatting | bytes 3670016 | tf_op jit(solution)/shard_map/all_to_all | solution.py:203
  217.2 2.9 %copy.74 = bf16[128,7168]{1,0:T(8,128)(2,1)} copy(bf16[128,7168]{0,1:T(8,128)(2,1)S(1)} %bitcast.312) | data formatting | bytes 3670016
  220.1 2.3 all-reduce.2.cloned.1.call-done
  222.4 6.1 %copy.127 = bf16[640,5120]{1,0:T(8,128)(2,1)} copy(bf16[640,5120]{1,0:T(8,128)(2,1)} %all-reduce.2.cloned.1.call-done) | data formatting | bytes 13107200
  (118 shorter events, 31.5 us)
Async XLA Ops:
  7.2 78.5 %all-gather.2.cloned.1.call-start = ((), (), s32[]{:S(2)}) async-start(), calls=%async_computation.2 | async-start | bytes 11796480 | tf_op jit(solution)/shard_map/all_gather | solution.py:108
  11.8 6.0 %copy-start.3 = (s32[1,8]{1,0:T(1,128)S(1)}, s32[1,8]{1,0:T(1,128)}, u32[]{:S(2)}) copy-start(s32[1,8]{1,0:T(1,128)} %param.26) | copy-start | bytes 100
  11.8 42.6 %all-to-all-start = ((bf16[128,8,896]{0,2,1:T(8,128)(2,1)}), bf16[128,8,896]{0,2,1:T(8,128)(2,1)S(1)}, u32[]{:S(2)}, u32[]{:S(2)}) async-start(bf16[128,8,896]{0,2,1:T(8,128)(2,1)} %bitcast.310), calls=%async_computation | async-start | bytes 3670016 | tf_op jit(solution)/shard_map/all_to_all | solution.py:60
  17.7 204.7 %all-reduce.2.cloned.1.call-start = ((), (), s32[]{:S(2)}) async-start(), calls=%async_computation.3 | async-start | bytes 13107200 | tf_op jit(solution)/shard_map/psum | solution.py:117
  20.0 6.5 %copy-start.2 = (s32[1024]{0:T(1024)S(1)}, s32[1024]{0:T(1024)}, u32[]{:S(2)}) copy-start(s32[1024]{0:T(1024)} %param.27) | copy-start | bytes 12292
  62.8 1.2 copy-start.1
  182.7 1.2 copy-start
Sparse Core Ops, SparseCore 0:
  9.7 75.9 all-gather.1
  97.5 124.8 all-reduce.1

commit v5 on v4

--- a/solution.py
+++ b/solution.py
@@ -58,6 +58,7 @@
 def local(query_key_value_rows, cotangent, out_weight, parents, rollout_spans):
     queries_per_group = QUERY_HEADS // KEY_VALUE_HEADS
     head_rows = lax.all_to_all(query_key_value_rows, "ctx", split_axis=1, concat_axis=0, tiled=True)
+    cotangent, head_rows = lax.optimization_barrier((cotangent, head_rows))
     tree_len = head_rows.shape[0]
     kv_local = head_rows.shape[1] // ((queries_per_group + 2) * HEAD_SIZE)
     heads_local = kv_local * queries_per_group

time: 237 us -> 258 us (1.089)
  blocking collectives: 27 us -> 56.4 us
  starting transfers between devices: 5.97 us -> 0.08 us
  waiting for transfers between devices: 37.4 us -> 32.3 us
  local copies, waits for them, and re-layouts: 43.5 us -> 47.6 us
    all_to_all x0 -> x1, blocking collectives: none -> 29.4 us  [local(): lax.all_to_all(query_key_value_rows, 'ctx', split_axis=1, concat_axis=0,...]
    all_to_all x1 -> x0, waiting for transfers between devices: 27.9 us -> none  [local(): lax.all_to_all(query_key_value_rows, 'ctx', split_axis=1, concat_axis=0,...]
    all_gather x1, waiting for transfers between devices: 6.48 us -> 32.2 us  [local(): shard_rows = lax.all_gather(cotangent, 'ctx', axis=0, tiled=True)]
    all_to_all x1 -> x0, starting transfers between devices: 5.93 us -> none  [local(): lax.all_to_all(query_key_value_rows, 'ctx', split_axis=1, concat_axis=0,...]
    slice x1 -> x5, local copies, waits for them, and re-layouts: 0.74 us -> 4.96 us  [one_head(): own_rows = own_all[opening_slot:closing_slot]]
    optimization_barrier x0 -> x1, local copies, waits for them, and re-layouts: none -> 3 us  [local(): cotangent, head_rows = lax.optimization_barrier((cotangent, head_rows))]
    reshape x1 -> x0, local copies, waits for them, and re-layouts: 2.89 us -> none  [local(): head_rows.reshape(tree_len, kv_local, queries_per_group + 2, HEAD_SIZE)]
    unnamed x13 -> x12, local copies, waits for them, and re-layouts: 15.4 us -> 15.2 us
  transfers between devices with their start and end apart: 3 -> 2, of which waited for: 3 -> 1; matrix products, arithmetic and copies ran while one was open for 56% -> 50% of each run, Pallas kernels for 0% -> 0%
where the time goes in v5:
time: 258 us; the launch traced here: 256 us
  matrix products  89.1 us (35%)
  blocking collectives  56.4 us (22%)
  local copies, waits for them, and re-layouts  47.6 us (18%)
  waiting for transfers between devices  32.3 us (13%)
  other arithmetic  16.1 us (6%)
  between operations  14.3 us (6%)
    dot_general x21, matrix products, contract_cols(): lax.dot_general(left, right, (((1,), (1,)), ((), ())), preferred_element_...  39.5 us
    dot_general x21, matrix products, contract_rows(): lax.dot_general(left, right, (((0,), (0,)), ((), ())), preferred_element_...  38.2 us
    all_gather x1, waiting for transfers between devices, local(): shard_rows = lax.all_gather(cotangent, 'ctx', axis=0, tiled=True)  32.2 us
    all_to_all x1, blocking collectives, local(): lax.all_to_all(query_key_value_rows, 'ctx', split_axis=1, concat_axis=0,...  29.4 us
    all_to_all x1, blocking collectives, local(): lax.all_to_all(gradients, 'ctx', split_axis=0, concat_axis=1, tiled=True)  26.9 us
    unnamed x12, local copies, waits for them, and re-layouts  15.2 us
    reduce_sum x5, other arithmetic, one_head(): jnp.sum(grad_rows.astype(jnp.float32) * own_rows.astype(jnp.float32), axi...  5.97 us
  transfers between devices with their start and end apart: 2, of which 1 were waited for; matrix products, arithmetic and copies ran while one was open for 50% of the time, Pallas kernels for 0%

profile of v5, /device:TPU:1, one launch (start us, length us, event | category | flops | bytes accessed | tf_op | source)
XLA Modules:
  0.0 256.4 jit_solution(4620815039863929957)
XLA Ops:
  7.2 3.9 %copy.79 = bf16[128,7168]{0,1:T(8,128)(2,1)} copy(bf16[128,7168]{1,0:T(8,128)(2,1)} %param.23) | data formatting | bytes 3670016 | tf_op args[0]
  11.1 29.4 %all_to_all.38 = bf16[128,8,896]{0,2,1:T(8,128)(2,1)S(1)} all-to-all(bf16[128,8,896]{0,2,1:T(8,128)(2,1)} %bitcast.309), channel_id=1, replica_groups=mesh['leaf'=16,'ctx'=8] {'ctx'}, dimensions={1} | all-to-all | bytes 3670016 | tf_op jit(solution)/shard_map/all_to_all | solution.py:60
  40.5 2.6 %copy.80 = bf16[8,128,896]{2,1,0:T(8,128)(2,1)} copy(bf16[8,128,896]{1,2,0:T(8,128)(2,1)S(1)} %bitcast.306) | data formatting | bytes 3670016 | tf_op jit(solution)/shard_map/all_to_all | solution.py:60
  43.2 2.2 while.53
  45.5 1.6 broadcast_in_dim.151
  47.9 1.6 broadcast_in_dim.155
  50.4 1.6 copy.86
  52.0 3.0 %copy.81 = bf16[1024,896]{0,1:T(8,128)(2,1)S(1)} copy(bf16[1024,896]{1,0:T(8,128)(2,1)} %bitcast.305) | data formatting | bytes 3670016 | tf_op jit(solution)/shard_map/optimization_barrier | solution.py:61
  59.0 1.8 fusion.34
  60.8 2.2 exponential_reduce_fusion
  63.1 1.6 fusion.55
  64.7 3.2 %fusion.52 = bf16[512,1,5,128]{0,3,2,1:T(8,128)(2,1)S(1)} fusion(f32[1024,512,5]{1,0,2:T(8,128)S(1)} %get-tuple-element.640, f32[5,512]{1,0:T(8,128)S(1)} %log_add_fusion, f32[512]{0:T(512)S(1)} %get-tuple-element.638, pred[512,1024]{0,1:T(8,128)(4,1)S(1)} %copy-done.1, bf16[1024,1,7,128]{0,3,2,1:T(8,128)(2,1)S(1)} %bitcast.303), kind=kOutput, calls=%fused_computation.85 | convolution fusion | flops 681902080 | bytes 11945984 | tf_op jit(solution)/shard_map/gjts,sgd->tgjd/dot_general | solution.py:98
  67.9 1.9 fusion.77
  70.9 32.2 %all-gather.2.cloned.1.call-done = bf16[1024,5120]{1,0:T(8,128)(2,1)} async-done(((bf16[128,5120]{1,0:T(8,128)(2,1)}), bf16[1024,5120]{1,0:T(8,128)(2,1)}) %all-gather.2.cloned.1.call-update) | async-done | bytes 10485776 | tf_op jit(solution)/shard_map/all_gather | solution.py:109
  103.2 11.7 %convolution_convert_fusion.3 = bf16[640,5120]{1,0:T(8,128)(2,1)} fusion(bf16[1024,640]{0,1:T(8,128)(2,1)} %bitcast.314, bf16[1024,5120]{1,0:T(8,128)(2,1)} %all-gather.2.cloned.1.call-done), kind=kOutput, calls=%fused_computation.66 | convolution fusion | flops 6714163200 | bytes 18350080 | tf_op jit(solution)/shard_map/dot_general | solution.py:47
  114.9 91.2 %conditional.1 = (bf16[1024,896]{0,1:T(8,128)(2,1)S(1)}) conditional(s32[]{:T(128)} %convert_element_type.148, () %tuple.94, (bf16[1024,5120]{1,0:T(8,128)(2,1)}, bf16[640,5120]{1,0:T(8,128)(2,1)}, f32[1,5,1024]{2,1,0:T(8,128)S(1)}, bf16[5,1024,128]{1,2,0:T(8,128)(2,1)}, bf16[1024,1,128]{2,0,1:T(8,128)(2,1)S(1)}, /*index=5*/f32[1024]{0:T(1024)S(1)}, ...), branch_computations={%region_7.8_spmd, %region_8.13_spmd} | conditional | flops 7727873024 | bytes 53645708 | solution.py:203
  115.1 11.6 %convolution_convert_fusion.2 = bf16[1024,640]{0,1:T(8,128)(2,1)S(1)} fusion(bf16[1024,5120]{1,0:T(8,128)(2,1)} %get-tuple-element.479, bf16[640,5120]{1,0:T(8,128)(2,1)} %get-tuple-element.514), kind=kOutput, calls=%fused_computation.54 | convolution fusion | flops 6711541760 | bytes 18350080 | tf_op jit(solution)/shard_map/cond/branch_1_fun/dot_general | solution.py:53
  126.7 1.5 copy.75
  128.2 76.0 %while.52 = (s32[]{:T(128)}, f32[1024,1,128]{2,0,1:T(8,128)S(1)}, f32[1024,1,128]{2,0,1:T(8,128)S(1)}, bf16[5,1024,128]{1,2,0:T(8,128)(2,1)}, bf16[5,1024,128]{1...) while((s32[]{:T(128)}, f32[1024,1,128]{2,0,1:T(8,128)S(1)}, ...), condition=%wide.region_12.12_spmd, body=%wide.region_9.11_spmd.sunk | while | flops 1014496256 | bytes 25858292 | solution.py:176
  130.9 1.3 fusion.126
  132.2 1.3 fusion.131
  133.5 1.2 fusion.128
  134.7 1.3 fusion.129
  136.3 1.6 subtract_exponential_fusion.2
  137.9 1.4 fusion.132
  139.3 1.4 multiply_convert_fusion.2
  140.7 1.4 fusion.130
  146.1 1.3 fusion.126
  147.5 1.3 fusion.131
  148.7 1.2 fusion.128
  150.0 1.3 fusion.129
  151.5 1.6 subtract_exponential_fusion.2
  153.2 1.4 fusion.132
  154.6 1.4 multiply_convert_fusion.2
  155.9 1.4 fusion.130
  161.3 1.4 fusion.126
  162.7 1.3 fusion.131
  165.2 1.3 fusion.129
  166.7 1.6 subtract_exponential_fusion.2
  168.3 1.4 fusion.132
  169.7 1.4 multiply_convert_fusion.2
  171.1 1.4 fusion.130
  176.5 1.3 fusion.126
  177.9 1.3 fusion.131
  179.1 1.2 fusion.128
  180.4 1.3 fusion.129
  181.9 1.6 subtract_exponential_fusion.2
  183.5 1.4 fusion.132
  184.9 1.4 multiply_convert_fusion.2
  186.3 1.4 fusion.130
  191.7 1.4 fusion.126
  193.1 1.3 fusion.131
  194.3 1.2 fusion.128
  195.6 1.3 fusion.129
  197.1 1.6 subtract_exponential_fusion.2
  198.7 1.4 fusion.132
  200.1 1.4 multiply_convert_fusion.2
  201.5 1.4 fusion.130
  204.5 1.5 pad_maximum_fusion
  207.3 3.2 %copy.93 = bf16[1024,896]{1,0:T(8,128)(2,1)S(1)} copy(bf16[1024,896]{0,1:T(8,128)(2,1)} %copy-done) | data formatting | bytes 3670016 | tf_op jit(solution)/shard_map/cond | solution.py:203
  210.5 26.9 %all_to_all.39 = bf16[8,128,896]{2,1,0:T(8,128)(2,1)} all-to-all(bf16[8,128,896]{2,1,0:T(8,128)(2,1)S(1)} %bitcast.307), channel_id=1, replica_groups=mesh['leaf'=16,'ctx'=8] {'ctx'}, dimensions={0} | all-to-all | bytes 3670016 | tf_op jit(solution)/shard_map/all_to_all | solution.py:204
  237.5 3.2 %copy.94 = bf16[8,128,896]{1,2,0:T(8,128)(2,1)S(1)} copy(bf16[8,128,896]{2,1,0:T(8,128)(2,1)} %all_to_all.39) | data formatting | bytes 3670016 | tf_op jit(solution)/shard_map/all_to_all | solution.py:204
  240.6 2.9 %copy.95 = bf16[128,7168]{1,0:T(8,128)(2,1)} copy(bf16[128,7168]{0,1:T(8,128)(2,1)S(1)} %bitcast.308) | data formatting | bytes 3670016
  243.5 6.1 %copy.153 = bf16[640,5120]{1,0:T(8,128)(2,1)} copy(bf16[640,5120]{1,0:T(8,128)(2,1)} %all-reduce.2.cloned.1.call-done) | data formatting | bytes 13107200
  (131 shorter events, 33.1 us)
Async XLA Ops:
  7.2 96.0 %all-gather.2.cloned.1.call-start = ((), (), s32[]{:S(2)}) async-start(), calls=%async_computation.2 | async-start | bytes 11796480 | tf_op jit(solution)/shard_map/all_gather | solution.py:109
  40.5 2.7 %copy-start.3 = (s32[1,8]{1,0:T(1,128)S(1)}, s32[1,8]{1,0:T(1,128)}, u32[]{:S(2)}) copy-start(s32[1,8]{1,0:T(1,128)} %param.26) | copy-start | bytes 100
  43.2 200.4 %all-reduce.2.cloned.1.call-start = ((), (), s32[]{:S(2)}) async-start(), calls=%async_computation.3 | async-start | bytes 13107200 | tf_op jit(solution)/shard_map/psum | solution.py:118
  45.5 6.5 %copy-start.2 = (s32[1024]{0:T(1024)S(1)}, s32[1024]{0:T(1024)}, u32[]{:S(2)}) copy-start(s32[1024]{0:T(1024)} %param.27) | copy-start | bytes 12292
  57.9 1.1 copy-start.1
  206.1 1.2 copy-start
Sparse Core Ops, SparseCore 0:
  43.3 59.8 all-gather.1
  115.0 124.5 all-reduce.1
